TPU v7x, 32 devices: a whole 2x2x4 slice. The times are simulated.
32 devices in a mesh: sky: 8 (over z, y), los: 4 (over x, core).
Axes of the slice: x: 2, y: 2, z: 4, core: 2. Of those that a mesh axis runs over, the one named last changes fastest.
Arguments:
- features: bfloat16 [32, 16, 32, 128], P(None, 'sky', 'los'), may hold values from -6 to 6
- pre_first: bfloat16 [32, 16, 32, 128], P(None, 'sky', 'los'), may hold values from -8 to 8
- pre_second: bfloat16 [32, 16, 32, 128], P(None, 'sky', 'los'), may hold values from -8 to 8
- w_first: bfloat16 [3, 3, 3, 32, 32], replicated, may hold values from -0.21875 to 0.21875
- w_second: bfloat16 [3, 3, 3, 32, 32], replicated, may hold values from -0.21875 to 0.21875
- w_out: bfloat16 [3, 32], replicated, may hold values from -1 to 1
- b_out: float32 [3], replicated, may hold values from -1 to 1
- y_target: float32 [16, 128], P('sky'), may hold values from -6 to 6
- k_target: float32 [16, 128], P('sky'), may hold values from -6 to 6
Outputs:
- grad_features: bfloat16 [32, 16, 32, 128], P(None, 'sky', 'los')
- grad_first: float32 [3, 3, 3, 32, 32], replicated
- grad_second: float32 [3, 3, 3, 32, 32], replicated
- grad_out: float32 [3, 32], replicated
- grad_bias: float32 [3], replicated
All inputs are finite; a program needn't handle non-finite values.
Results may differ from a plain program's by a relative error of at most 0.0067.
Values may be sent and summed in bfloat16 or wider, within the bound.
No kernel may reach another device: no remote copies, remote signals or barrier semaphores. Data moves between devices by JAX's collectives and lax.ppermute only.
A program may use at most 64 MiB of HBM per device.

v0:
```python
import math

import jax
import jax.numpy as jnp
from jax import lax
from jax.sharding import PartitionSpec as P


def extended(block, sides, width):
    for axis, dim in sides:
        count = lax.axis_size(axis)
        forward = [(i, i + 1) for i in range(count - 1)]
        forward.append((count - 1, 0))
        backward = [(target, source) for source, target in forward]
        low = lax.ppermute(
            lax.slice_in_dim(block, block.shape[dim] - width, None, axis=dim), axis, forward
        )
        high = lax.ppermute(lax.slice_in_dim(block, 0, width, axis=dim), axis, backward)
        block = jnp.concatenate([low, block, high], axis=dim)
    return block


def silu_slope(value):
    sigma = jax.nn.sigmoid(value)
    return sigma * (1.0 + value * (1.0 - sigma))


def wrap_columns(field):
    return jnp.concatenate((field[..., -1:], field, field[..., :1]), axis=-1)


def spread_local(weight, padded, shape):
    result = jnp.zeros(shape, jnp.float32)
    for tap_x in range(3):
        for tap_z in range(3):
            for tap_y in range(3):
                window = padded[
                    :,
                    2 - tap_x : 2 - tap_x + shape[1],
                    2 - tap_z : 2 - tap_z + shape[2],
                    2 - tap_y : 2 - tap_y + shape[3],
                ]
                result = result + jnp.einsum(
                    "oi,oxzy->ixzy",
                    weight[tap_x, tap_z, tap_y],
                    window,
                    preferred_element_type=jnp.float32,
                )
    return result


def taps_from_inputs(grad_field, padded_inputs):
    shape = grad_field.shape
    taps_list = []
    for tap_x in range(3):
        for tap_z in range(3):
            for tap_y in range(3):
                window = padded_inputs[
                    :, tap_x : tap_x + shape[1], tap_z : tap_z + shape[2], tap_y : tap_y + shape[3]
                ]
                taps_list.append(
                    jnp.einsum(
                        "oxzy,ixzy->oi", grad_field, window, preferred_element_type=jnp.float32
                    )
                )
    return jnp.stack(taps_list).reshape(3, 3, 3, shape[0], padded_inputs.shape[0])


def per_device(
    features, pre_first, pre_second, w_first, w_second, w_out, b_out, y_target, k_target
):
    count_sky = lax.axis_size("sky")
    count_los = lax.axis_size("los")
    depth_all = pre_first.shape[2] * count_los
    norm_factor = 1.0 / math.sqrt(features.shape[1] * count_sky * features.shape[3] * depth_all)
    shape = features.shape
    first_wide = pre_first.astype(jnp.float32)
    second_wide = pre_second.astype(jnp.float32)
    hidden_second = jax.nn.silu(second_wide).astype(jnp.bfloat16)
    heads_raw = jnp.einsum(
        "oi,ixzy->oxzy", w_out, hidden_second, preferred_element_type=jnp.float32
    )
    heads_raw = heads_raw + b_out[:, None, None, None]
    pressure = jax.nn.softplus(heads_raw[0])
    density = jax.nn.softplus(heads_raw[1])
    velocity = heads_raw[2]
    y_part = jnp.sum(pressure, axis=1) / depth_all
    k_part = -jnp.sum(density * velocity, axis=1) / depth_all
    y_map, k_map = lax.psum((y_part, k_part), "los")
    y_resid = y_map - y_target
    k_resid = k_map - k_target
    y_resid = y_resid[:, None, :]
    k_resid = k_resid[:, None, :]
    head_grad = jnp.stack(
        (
            y_resid * jax.nn.sigmoid(heads_raw[0]),
            -k_resid * velocity * jax.nn.sigmoid(heads_raw[1]),
            -k_resid * density,
        )
    ).astype(jnp.bfloat16)
    grad_out = (
        jnp.einsum("oxzy,ixzy->oi", head_grad, hidden_second, preferred_element_type=jnp.float32)
        * norm_factor
    )
    grad_bias = jnp.sum(head_grad.astype(jnp.float32), axis=(1, 2, 3)) * norm_factor
    back_second = jnp.einsum("oi,oxzy->ixzy", w_out, head_grad, preferred_element_type=jnp.float32)
    grad_second_pre = (back_second * silu_slope(second_wide)).astype(jnp.bfloat16)
    second_padded = wrap_columns(extended(grad_second_pre, (("sky", 1), ("los", 2)), 1))
    back_first = spread_local(w_second, second_padded, shape)
    grad_first_pre = (back_first * silu_slope(first_wide)).astype(jnp.bfloat16)
    first_padded = wrap_columns(extended(grad_first_pre, (("sky", 1), ("los", 2)), 1))
    grad_features = spread_local(w_first, first_padded, shape).astype(jnp.bfloat16)
    saved_padded = wrap_columns(
        extended(jnp.stack((features, pre_first)), (("sky", 2), ("los", 3)), 1)
    )
    hidden_padded = jax.nn.silu(saved_padded[1].astype(jnp.float32)).astype(jnp.bfloat16)
    grad_second = taps_from_inputs(grad_second_pre, hidden_padded)
    grad_first = taps_from_inputs(grad_first_pre, saved_padded[0])
    grad_first, grad_second, grad_out, grad_bias = lax.psum(
        (grad_first * norm_factor, grad_second * norm_factor, grad_out, grad_bias), ("sky", "los")
    )
    return (grad_features, grad_first, grad_second, grad_out, grad_bias)


def solution(mesh):
    in_specs = (
        P(None, "sky", "los", None),
        P(None, "sky", "los", None),
        P(None, "sky", "los", None),
        P(),
        P(),
        P(),
        P(),
        P("sky", None),
        P("sky", None),
    )
    out_specs = (P(None, "sky", "los", None), P(), P(), P(), P())
    return jax.shard_map(
        per_device, mesh=mesh, in_specs=in_specs, out_specs=out_specs, check_vma=False
    )
```

profile of v0, /device:TPU:0, one launch (start us, length us, event | category | flops | bytes accessed | tf_op | source)
XLA Modules:
  0.0 245.4 jit_solution(12712252060760157756)
XLA Ops:
  7.3 1.0 copy.311
  8.2 0.9 copy.312
  9.2 3.0 %collective-permute-start.8 = (bf16[2,32,1,8,128]{4,1,3,2,0:T(8,128)(2,1)S(1)}, bf16[2,32,1,8,128]{4,1,3,2,0:T(8,128)(2,1)S(1)}, u32[]{:S(2)}, u32[]{:S(2)}) collective-permute-start(bf16[2,32,1,8,128]{4,1,3,2,0:T(8,128)(2,1)S(1)} %get-tuple-element.37), channel_id=1, source_target_pairs={{0,4},{4,8},{8,12},{12,16},{16,20},{20,24},{24,28},{28,0},{1,5},{5... | collective-permute-start | bytes 393224 | tf_op jit(solution)/shard_map/ppermute | solution.py:15
  12.2 3.1 %collective-permute-start.9 = (bf16[2,32,1,8,128]{4,1,3,2,0:T(8,128)(2,1)S(1)}, bf16[2,32,1,8,128]{4,1,3,2,0:T(8,128)(2,1)S(1)}, u32[]{:S(2)}, u32[]{:S(2)}) collective-permute-start(bf16[2,32,1,8,128]{4,1,3,2,0:T(8,128)(2,1)S(1)} %get-tuple-element.38), channel_id=1, source_target_pairs={{4,0},{8,4},{12,8},{16,12},{20,16},{24,20},{28,24},{0,28},{5,1},{9... | collective-permute-start | bytes 393224 | tf_op jit(solution)/shard_map/ppermute | solution.py:18
  15.3 1.0 fusion.100
  16.6 6.3 %all-reduce.2 = (f32[2,128]{1,0:T(2,128)S(1)}, f32[2,128]{1,0:T(2,128)S(1)}) all-reduce(f32[2,128]{1,0:T(2,128)S(1)} %get-tuple-element.54, f32[2,128]{1,0:T(2,128)S(1)} %get-tuple-element.55), channel_id=1, replica_groups=mesh['sky'=8,'los'=4] {'los'}, use_global_device_ids=true, to_apply=%region_3.4 | all-reduce | flops 512 | bytes 4096 | tf_op jit(solution)/shard_map/psum | solution.py:89
  23.4 4.7 %collective-permute-start.1 = (bf16[32,1,8,128]{3,0,2,1:T(8,128)(2,1)S(1)}, bf16[32,1,8,128]{3,0,2,1:T(8,128)(2,1)S(1)}, u32[]{:S(2)}, u32[]{:S(2)}) collective-permute-start(bf16[32,1,8,128]{3,0,2,1:T(8,128)(2,1)S(1)} %get-tuple-element.50), channel_id=1, source_target_pairs={{4,0},{8,4},{12,8},{16,12},{20,16},{24,20},{28,24},{0,28},{5,1},{9... | collective-permute-start | bytes 196616 | tf_op jit(solution)/shard_map/ppermute | solution.py:18
  28.2 2.1 collective-permute-done
  30.4 1.7 collective-permute-start.3
  32.2 39.6 %all-reduce = (f32[3,32]{1,0:T(4,128)}, f32[3]{0:T(128)}) all-reduce(f32[3,32]{1,0:T(4,128)S(1)} %fusion.91, f32[3]{0:T(128)S(1)} %broadcast_multiply_fusion.3), channel_id=1, replica_groups=mesh['sky'=8,'los'=4] {'sky','los'}, use_global_device_ids=true, to_apply=%region_6.7 | all-reduce | flops 99 | bytes 792 | tf_op jit(solution)/shard_map/psum | solution.py:119
  72.0 0.5 pad_maximum_fusion.1
  79.4 2.6 %collective-permute-start.4 = (bf16[32,1,8,128]{3,0,2,1:T(8,128)(2,1)S(1)}, bf16[32,1,8,128]{3,0,2,1:T(8,128)(2,1)S(1)}, u32[]{:S(2)}, u32[]{:S(2)}) collective-permute-start(bf16[32,1,8,128]{3,0,2,1:T(8,128)(2,1)S(1)} %get-tuple-element.47), channel_id=1, source_target_pairs={{0,4},{4,8},{8,12},{12,16},{16,20},{20,24},{24,28},{28,0},{1,5},{5... | collective-permute-start | bytes 196616 | tf_op jit(solution)/shard_map/ppermute | solution.py:15
  82.0 2.2 collective-permute-start.5
  84.3 1.7 collective-permute-start.11
  86.0 0.5 collective-permute-done.4
  87.1 1.7 collective-permute-start.7
  89.2 0.8 pad_maximum_fusion
  96.4 0.8 broadcast_multiply_fusion
  103.2 0.8 broadcast_multiply_fusion.1
  104.3 0.5 pad_maximum_fusion.2
  111.4 0.7 copy.134
  112.1 122.8 %all-reduce.5.cloned.1.call-done = (f32[3,3,3,32,32]{4,3,2,1,0:T(8,128)}, f32[3,3,3,32,32]{4,3,2,1,0:T(8,128)}) async-done(((f32[3,3,3,32,32]{4,3,2,1,0:T(8,128)}, f32[3,3,3,32,32]{4,3,2,1,0:T(8,128)}), (f32[3,3,3,32,32]{4,3,2,1,0:T(8,128)}, f32[3,3,3,32,32]{4,3,2,1,0:T(8,128)})) %all-reduce.5.cloned.1.call-update) | async-done | bytes 221200 | tf_op jit(solution)/shard_map/psum | solution.py:119
  235.0 1.8 copy.367
  236.8 1.8 copy.368
  (167 shorter events, 27.9 us)
Async XLA Ops:
  7.2 9.2 %copy-start = (bf16[3,32]{1,0:T(4,128)(2,1)S(1)}, bf16[3,32]{1,0:T(4,128)(2,1)}, u32[]{:S(2)}) copy-start(bf16[3,32]{1,0:T(4,128)(2,1)} %param.14) | copy-start | bytes 580
  7.2 15.9 %copy-start.3 = (bf16[32,2,8,128]{3,2,1,0:T(8,128)(2,1)S(1)}, bf16[32,2,8,128]{3,2,1,0:T(8,128)(2,1)}, u32[]{:S(2)}) copy-start(bf16[32,2,8,128]{3,2,1,0:T(8,128)(2,1)} %param.11) | copy-start | bytes 393220
  7.2 9.3 %copy-start.7 = (f32[3]{0:T(128)S(1)}, f32[3]{0:T(128)}, u32[]{:S(2)}) copy-start(f32[3]{0:T(128)} %param.15) | copy-start | bytes 40
  7.2 15.7 %copy-start.5 = (f32[2,128]{1,0:T(2,128)S(1)}, f32[2,128]{1,0:T(2,128)}, u32[]{:S(2)}) copy-start(f32[2,128]{1,0:T(2,128)} %param.16) | copy-start | bytes 3076
  7.2 15.7 %copy-start.6 = (f32[2,128]{1,0:T(2,128)S(1)}, f32[2,128]{1,0:T(2,128)}, u32[]{:S(2)}) copy-start(f32[2,128]{1,0:T(2,128)} %param.17) | copy-start | bytes 3076
  7.2 227.8 %all-reduce.5.cloned.1.call-start = ((), (), s32[]{:S(2)}) async-start(), calls=%async_computation | async-start | bytes 1769472 | tf_op jit(solution)/shard_map/psum | solution.py:119
  9.2 75.0 %collective-permute-start.8 = (bf16[2,32,1,8,128]{4,1,3,2,0:T(8,128)(2,1)S(1)}, bf16[2,32,1,8,128]{4,1,3,2,0:T(8,128)(2,1)S(1)}, u32[]{:S(2)}, u32[]{:S(2)}) collective-permute-start(bf16[2,32,1,8,128]{4,1,3,2,0:T(8,128)(2,1)S(1)} %get-tuple-element.37), channel_id=1, source_target_pairs={{0,4},{4,8},{8,12},{12,16},{16,20},{20,24},{24,28},{28,0},{1,5},{5... | collective-permute-start | bytes 393224 | tf_op jit(solution)/shard_map/ppermute | solution.py:15
  12.2 72.0 %collective-permute-start.9 = (bf16[2,32,1,8,128]{4,1,3,2,0:T(8,128)(2,1)S(1)}, bf16[2,32,1,8,128]{4,1,3,2,0:T(8,128)(2,1)S(1)}, u32[]{:S(2)}, u32[]{:S(2)}) collective-permute-start(bf16[2,32,1,8,128]{4,1,3,2,0:T(8,128)(2,1)S(1)} %get-tuple-element.38), channel_id=1, source_target_pairs={{4,0},{8,4},{12,8},{16,12},{20,16},{24,20},{28,24},{0,28},{5,1},{9... | collective-permute-start | bytes 393224 | tf_op jit(solution)/shard_map/ppermute | solution.py:18
  23.3 7.0 %collective-permute-start = (bf16[32,1,8,128]{3,0,2,1:T(8,128)(2,1)S(1)}, bf16[32,1,8,128]{3,0,2,1:T(8,128)(2,1)S(1)}, u32[]{:S(2)}, u32[]{:S(2)}) collective-permute-start(bf16[32,1,8,128]{3,0,2,1:T(8,128)(2,1)S(1)} %get-tuple-element.49), channel_id=1, source_target_pairs={{0,4},{4,8},{8,12},{12,16},{16,20},{20,24},{24,28},{28,0},{1,5},{5... | collective-permute-start | bytes 196616 | tf_op jit(solution)/shard_map/ppermute | solution.py:15
  23.4 7.0 %collective-permute-start.1 = (bf16[32,1,8,128]{3,0,2,1:T(8,128)(2,1)S(1)}, bf16[32,1,8,128]{3,0,2,1:T(8,128)(2,1)S(1)}, u32[]{:S(2)}, u32[]{:S(2)}) collective-permute-start(bf16[32,1,8,128]{3,0,2,1:T(8,128)(2,1)S(1)} %get-tuple-element.50), channel_id=1, source_target_pairs={{4,0},{8,4},{12,8},{16,12},{20,16},{24,20},{28,24},{0,28},{5,1},{9... | collective-permute-start | bytes 196616 | tf_op jit(solution)/shard_map/ppermute | solution.py:18
  30.4 41.4 %collective-permute-start.2 = (bf16[32,4,1,128]{3,0,2,1:T(8,128)(2,1)S(1)}, bf16[32,4,1,128]{3,0,2,1:T(8,128)(2,1)S(1)}, u32[]{:S(2)}, u32[]{:S(2)}) collective-permute-start(bf16[32,4,1,128]{3,0,2,1:T(8,128)(2,1)S(1)} %get-tuple-element.45), channel_id=1, source_target_pairs={{0,1},{1,2},{2,3},{3,0},{4,5},{5,6},{6,7},{7,4},{8,9},{9,10},{10,1... | collective-permute-start | bytes 98312 | tf_op jit(solution)/shard_map/ppermute | solution.py:15
  30.4 41.4 %collective-permute-start.3 = (bf16[32,4,1,128]{3,0,2,1:T(8,128)(2,1)S(1)}, bf16[32,4,1,128]{3,0,2,1:T(8,128)(2,1)S(1)}, u32[]{:S(2)}, u32[]{:S(2)}) collective-permute-start(bf16[32,4,1,128]{3,0,2,1:T(8,128)(2,1)S(1)} %get-tuple-element.46), channel_id=1, source_target_pairs={{1,0},{2,1},{3,2},{0,3},{5,4},{6,5},{7,6},{4,7},{9,8},{10,9},{11,1... | collective-permute-start | bytes 98312 | tf_op jit(solution)/shard_map/ppermute | solution.py:18
  72.0 0.9 copy-start.2
  78.3 0.9 copy-start.4
  79.4 7.1 %collective-permute-start.4 = (bf16[32,1,8,128]{3,0,2,1:T(8,128)(2,1)S(1)}, bf16[32,1,8,128]{3,0,2,1:T(8,128)(2,1)S(1)}, u32[]{:S(2)}, u32[]{:S(2)}) collective-permute-start(bf16[32,1,8,128]{3,0,2,1:T(8,128)(2,1)S(1)} %get-tuple-element.47), channel_id=1, source_target_pairs={{0,4},{4,8},{8,12},{12,16},{16,20},{20,24},{24,28},{28,0},{1,5},{5... | collective-permute-start | bytes 196616 | tf_op jit(solution)/shard_map/ppermute | solution.py:15
  82.0 5.0 %collective-permute-start.5 = (bf16[32,1,8,128]{3,0,2,1:T(8,128)(2,1)S(1)}, bf16[32,1,8,128]{3,0,2,1:T(8,128)(2,1)S(1)}, u32[]{:S(2)}, u32[]{:S(2)}) collective-permute-start(bf16[32,1,8,128]{3,0,2,1:T(8,128)(2,1)S(1)} %get-tuple-element.48), channel_id=1, source_target_pairs={{4,0},{8,4},{12,8},{16,12},{20,16},{24,20},{28,24},{0,28},{5,1},{9... | collective-permute-start | bytes 196616 | tf_op jit(solution)/shard_map/ppermute | solution.py:18
  84.2 4.6 %collective-permute-start.10 = (bf16[2,32,4,1,128]{4,1,3,2,0:T(8,128)(2,1)S(1)}, bf16[2,32,4,1,128]{4,1,3,2,0:T(8,128)(2,1)S(1)}, u32[]{:S(2)}, u32[]{:S(2)}) collective-permute-start(bf16[2,32,4,1,128]{4,1,3,2,0:T(8,128)(2,1)S(1)} %get-tuple-element.27), channel_id=1, source_target_pairs={{0,1},{1,2},{2,3},{3,0},{4,5},{5,6},{6,7},{7,4},{8,9},{9,10},{10,1... | collective-permute-start | bytes 196616 | tf_op jit(solution)/shard_map/ppermute | solution.py:15
  84.3 4.5 %collective-permute-start.11 = (bf16[2,32,4,1,128]{4,1,3,2,0:T(8,128)(2,1)S(1)}, bf16[2,32,4,1,128]{4,1,3,2,0:T(8,128)(2,1)S(1)}, u32[]{:S(2)}, u32[]{:S(2)}) collective-permute-start(bf16[2,32,4,1,128]{4,1,3,2,0:T(8,128)(2,1)S(1)} %get-tuple-element.28), channel_id=1, source_target_pairs={{1,0},{2,1},{3,2},{0,3},{5,4},{6,5},{7,6},{4,7},{9,8},{10,9},{11,1... | collective-permute-start | bytes 196616 | tf_op jit(solution)/shard_map/ppermute | solution.py:18
  87.0 17.0 %collective-permute-start.6 = (bf16[32,4,1,128]{3,0,2,1:T(8,128)(2,1)S(1)}, bf16[32,4,1,128]{3,0,2,1:T(8,128)(2,1)S(1)}, u32[]{:S(2)}, u32[]{:S(2)}) collective-permute-start(bf16[32,4,1,128]{3,0,2,1:T(8,128)(2,1)S(1)} %get-tuple-element.41), channel_id=1, source_target_pairs={{0,1},{1,2},{2,3},{3,0},{4,5},{5,6},{6,7},{7,4},{8,9},{9,10},{10,1... | collective-permute-start | bytes 98312 | tf_op jit(solution)/shard_map/ppermute | solution.py:15
  87.1 16.9 %collective-permute-start.7 = (bf16[32,4,1,128]{3,0,2,1:T(8,128)(2,1)S(1)}, bf16[32,4,1,128]{3,0,2,1:T(8,128)(2,1)S(1)}, u32[]{:S(2)}, u32[]{:S(2)}) collective-permute-start(bf16[32,4,1,128]{3,0,2,1:T(8,128)(2,1)S(1)} %get-tuple-element.42), channel_id=1, source_target_pairs={{1,0},{2,1},{3,2},{0,3},{5,4},{6,5},{7,6},{4,7},{9,8},{10,9},{11,1... | collective-permute-start | bytes 98312 | tf_op jit(solution)/shard_map/ppermute | solution.py:18
  104.3 0.9 copy-start.1
Sparse Core Ops, SparseCore 0:
  104.1 130.8 all-reduce.4
where the time goes:
time: 246 us; the launch traced here: 245 us
  waiting for transfers between devices  126 us (51%)
  blocking collectives  45.9 us (19%)
  matrix products  24.4 us (10%)
  starting transfers between devices  21.1 us (9%)
  between operations  14.7 us (6%)
  local copies, waits for them, and re-layouts  8.01 us (3%)
  other arithmetic  5.42 us (2%)
    psum x1, waiting for transfers between devices, per_device(): lax.psum((grad_first * norm_factor, grad_second * norm_factor, grad_out,...  123 us
    psum x1, blocking collectives, per_device(): lax.psum((grad_first * norm_factor, grad_second * norm_factor, grad_out,...  39.6 us
    ppermute x6, starting transfers between devices, extended(): lax.ppermute(lax.slice_in_dim(block, 0, width, axis=dim), axis, backward)  15.2 us
    dot_general x54, matrix products, spread_local(): jnp.einsum('oi,oxzy->ixzy', weight[tap_x, tap_z, tap_y], window, preferre...  12 us
    dot_general x54, matrix products, taps_from_inputs(): jnp.einsum('oxzy,ixzy->oi', grad_field, window, preferred_element_type=jn...  11.9 us
    unnamed x21, local copies, waits for them, and re-layouts  7.35 us
    psum x1, blocking collectives, per_device(): y_map, k_map = lax.psum((y_part, k_part), 'los')  6.31 us
    ppermute x6, starting transfers between devices, extended(): lax.ppermute(lax.slice_in_dim(block, block.shape[dim] - width, None, axis...  5.83 us
  transfers between devices with their start and end apart: 13, of which 4 were waited for; matrix products, arithmetic and copies ran while one was open for 13% of the time, Pallas kernels for 0%

commit v1 on v0

--- a/solution.py
+++ b/solution.py
@@ -18,6 +18,38 @@
         high = lax.ppermute(lax.slice_in_dim(block, 0, width, axis=dim), axis, backward)
         block = jnp.concatenate([low, block, high], axis=dim)
     return block
+
+
+def butterfly_sum(value, axes):
+    for axis in axes:
+        count = lax.axis_size(axis)
+        if count & (count - 1):
+            value = lax.psum(value, axis)
+            continue
+        step = 1
+        while step < count:
+            pairs = [(i, i ^ step) for i in range(count)]
+            value = value + lax.ppermute(value, axis, pairs)
+            step *= 2
+    return value
+
+
+def pack_rows(parts):
+    flat = jnp.concatenate([part.reshape(-1) for part in parts])
+    rows = -(-flat.shape[0] // 128)
+    flat = jnp.pad(flat, (0, rows * 128 - flat.shape[0]))
+    return flat.reshape(rows, 128)
+
+
+def unpack_rows(packed, shapes):
+    flat = packed.reshape(-1)
+    parts = []
+    start = 0
+    for shape in shapes:
+        size = math.prod(shape)
+        parts.append(flat[start : start + size].reshape(shape))
+        start += size
+    return parts
 
 
 def silu_slope(value):
@@ -86,7 +118,7 @@
     velocity = heads_raw[2]
     y_part = jnp.sum(pressure, axis=1) / depth_all
     k_part = -jnp.sum(density * velocity, axis=1) / depth_all
-    y_map, k_map = lax.psum((y_part, k_part), "los")
+    y_map, k_map = butterfly_sum(jnp.stack((y_part, k_part)), ("los",))
     y_resid = y_map - y_target
     k_resid = k_map - k_target
     y_resid = y_resid[:, None, :]
@@ -116,9 +148,12 @@
     hidden_padded = jax.nn.silu(saved_padded[1].astype(jnp.float32)).astype(jnp.bfloat16)
     grad_second = taps_from_inputs(grad_second_pre, hidden_padded)
     grad_first = taps_from_inputs(grad_first_pre, saved_padded[0])
-    grad_first, grad_second, grad_out, grad_bias = lax.psum(
-        (grad_first * norm_factor, grad_second * norm_factor, grad_out, grad_bias), ("sky", "los")
+    early = (grad_second * norm_factor, grad_out, grad_bias)
+    early_shapes = [part.shape for part in early]
+    grad_second, grad_out, grad_bias = unpack_rows(
+        butterfly_sum(pack_rows(early), ("los", "sky")), early_shapes
     )
+    grad_first = butterfly_sum(grad_first * norm_factor, ("los", "sky"))
     return (grad_features, grad_first, grad_second, grad_out, grad_bias)
 
 

time: 246 us -> 126 us (0.51)
  waiting for transfers between devices: 126 us -> 65.8 us
  blocking collectives: 45.9 us -> 0 us
  between operations: 14.7 us -> 1.46 us
    psum x1 -> x0, waiting for transfers between devices: 123 us -> none  [per_device(): lax.psum((grad_first * norm_factor, grad_second * norm_factor, grad_out,...]
    ppermute x0 -> x12, waiting for transfers between devices: none -> 51.8 us  [butterfly_sum(): value = value + lax.ppermute(value, axis, pairs)]
    psum x2 -> x0, blocking collectives: 45.9 us -> none  [the longest x1 39.6 us: per_device(): lax.psum((grad_first * norm_factor, grad_second * norm_factor, grad_out,...]
    ppermute x0 -> x12, starting transfers between devices: none -> 8.24 us  [butterfly_sum(): value = value + lax.ppermute(value, axis, pairs)]
    ppermute x6, waiting for transfers between devices: 2.62 us -> 9.45 us  [extended(): lax.ppermute(lax.slice_in_dim(block, block.shape[dim] - width, None, axis...]
    ppermute x6, starting transfers between devices: 15.2 us -> 9.61 us  [extended(): lax.ppermute(lax.slice_in_dim(block, 0, width, axis=dim), axis, backward)]
    ppermute x6, waiting for transfers between devices: 0.44 us -> 4.6 us  [extended(): lax.ppermute(lax.slice_in_dim(block, 0, width, axis=dim), axis, backward)]
    unnamed x21 -> x17, local copies, waits for them, and re-layouts: 7.35 us -> 3.7 us
  transfers between devices with their start and end apart: 13 -> 24, of which waited for: 4 -> 14; matrix products, arithmetic and copies ran while one was open for 13% -> 25% of each run, Pallas kernels for 0% -> 0%
where the time goes in v1:
time: 126 us
  waiting for transfers between devices  65.8 us (52%)
  matrix products  24.3 us (19%)
  starting transfers between devices  21.4 us (17%)
  local copies, waits for them, and re-layouts  6.92 us (5%)
  other arithmetic  5.75 us (5%)
  between operations  1.46 us (1%)
    ppermute x12, waiting for transfers between devices, butterfly_sum(): value = value + lax.ppermute(value, axis, pairs)  51.8 us
    dot_general x54, matrix products, spread_local(): jnp.einsum('oi,oxzy->ixzy', weight[tap_x, tap_z, tap_y], window, preferre...  12 us
    dot_general x54, matrix products, taps_from_inputs(): jnp.einsum('oxzy,ixzy->oi', grad_field, window, preferred_element_type=jn...  11.8 us
    ppermute x6, starting transfers between devices, extended(): lax.ppermute(lax.slice_in_dim(block, 0, width, axis=dim), axis, backward)  9.61 us
    ppermute x6, waiting for transfers between devices, extended(): lax.ppermute(lax.slice_in_dim(block, block.shape[dim] - width, None, axis...  9.45 us
    ppermute x12, starting transfers between devices, butterfly_sum(): value = value + lax.ppermute(value, axis, pairs)  8.24 us
    ppermute x6, waiting for transfers between devices, extended(): lax.ppermute(lax.slice_in_dim(block, 0, width, axis=dim), axis, backward)  4.6 us
    unnamed x17, local copies, waits for them, and re-layouts  3.7 us
  transfers between devices with their start and end apart: 24, of which 14 were waited for; matrix products, arithmetic and copies ran while one was open for 25% of the time, Pallas kernels for 0%

profile of v1, /device:TPU:0, one launch (start us, length us, event | category | flops | bytes accessed | tf_op | source)
XLA Modules:
  0.0 125.6 jit_solution(14989581067133855482)
XLA Ops:
  0.7 1.0 fusion.100
  3.2 0.9 copy.370
  4.1 0.9 copy.371
  5.1 2.6 %collective-permute-start.1 = (f32[2,2,128]{2,1,0:T(2,128)S(1)}, f32[2,2,128]{2,1,0:T(2,128)S(1)}, u32[]{:S(2)}, u32[]{:S(2)}) collective-permute-start(f32[2,2,128]{2,1,0:T(2,128)S(1)} %fusion.352), channel_id=1, source_target_pairs={{0,2},{1,3},{2,0},{3,1},{4,6},{5,7},{6,4},{7,5},{8,10},{9,11},{10,... | collective-permute-start | bytes 6152 | tf_op jit(solution)/shard_map/ppermute | solution.py:32
  7.7 4.6 %collective-permute-start.11 = (bf16[2,32,1,8,128]{4,1,3,2,0:T(8,128)(2,1)S(1)}, bf16[2,32,1,8,128]{4,1,3,2,0:T(8,128)(2,1)S(1)}, u32[]{:S(2)}, u32[]{:S(2)}) collective-permute-start(bf16[2,32,1,8,128]{4,1,3,2,0:T(8,128)(2,1)S(1)} %get-tuple-element.37), channel_id=1, source_target_pairs={{4,0},{8,4},{12,8},{16,12},{20,16},{24,20},{28,24},{0,28},{5,1},{9... | collective-permute-start | bytes 393224 | tf_op jit(solution)/shard_map/ppermute | solution.py:18
  12.7 4.8 %collective-permute-start.3 = (bf16[32,1,8,128]{3,0,2,1:T(8,128)(2,1)S(1)}, bf16[32,1,8,128]{3,0,2,1:T(8,128)(2,1)S(1)}, u32[]{:S(2)}, u32[]{:S(2)}) collective-permute-start(bf16[32,1,8,128]{3,0,2,1:T(8,128)(2,1)S(1)} %get-tuple-element.49), channel_id=1, source_target_pairs={{4,0},{8,4},{12,8},{16,12},{20,16},{24,20},{28,24},{0,28},{5,1},{9... | collective-permute-start | bytes 196616 | tf_op jit(solution)/shard_map/ppermute | solution.py:18
  17.6 1.8 %collective-permute-done.3 = bf16[32,1,8,128]{3,0,2,1:T(8,128)(2,1)S(1)} collective-permute-done((bf16[32,1,8,128]{3,0,2,1:T(8,128)(2,1)S(1)}, bf16[32,1,8,128]{3,0,2,1:T(8,128)(2,1)S(1)}, u32[]{:S(2)}, u32[]{:S(2)}) %collective-permute-start.3) | collective-permute-done | bytes 65568 | tf_op jit(solution)/shard_map/ppermute | solution.py:18
  19.4 5.1 %collective-permute-done.2 = bf16[32,1,8,128]{3,0,2,1:T(8,128)(2,1)S(1)} collective-permute-done((bf16[32,1,8,128]{3,0,2,1:T(8,128)(2,1)S(1)}, bf16[32,1,8,128]{3,0,2,1:T(8,128)(2,1)S(1)}, u32[]{:S(2)}, u32[]{:S(2)}) %collective-permute-start.2) | collective-permute-done | bytes 65568 | tf_op jit(solution)/shard_map/ppermute | solution.py:15
  25.1 1.2 collective-permute-done.5
  26.3 1.6 %collective-permute-done.4 = bf16[32,4,1,128]{3,0,2,1:T(8,128)(2,1)S(1)} collective-permute-done((bf16[32,4,1,128]{3,0,2,1:T(8,128)(2,1)S(1)}, bf16[32,4,1,128]{3,0,2,1:T(8,128)(2,1)S(1)}, u32[]{:S(2)}, u32[]{:S(2)}) %collective-permute-start.4) | collective-permute-done | bytes 32800 | tf_op jit(solution)/shard_map/ppermute | solution.py:15
  35.6 2.0 %collective-permute-start.6 = (bf16[32,1,8,128]{3,0,2,1:T(8,128)(2,1)S(1)}, bf16[32,1,8,128]{3,0,2,1:T(8,128)(2,1)S(1)}, u32[]{:S(2)}, u32[]{:S(2)}) collective-permute-start(bf16[32,1,8,128]{3,0,2,1:T(8,128)(2,1)S(1)} %get-tuple-element.46), channel_id=1, source_target_pairs={{0,4},{4,8},{8,12},{12,16},{16,20},{20,24},{24,28},{28,0},{1,5},{5... | collective-permute-start | bytes 196616 | tf_op jit(solution)/shard_map/ppermute | solution.py:15
  38.2 1.7 %collective-permute-done.7 = bf16[32,1,8,128]{3,0,2,1:T(8,128)(2,1)S(1)} collective-permute-done((bf16[32,1,8,128]{3,0,2,1:T(8,128)(2,1)S(1)}, bf16[32,1,8,128]{3,0,2,1:T(8,128)(2,1)S(1)}, u32[]{:S(2)}, u32[]{:S(2)}) %collective-permute-start.7) | collective-permute-done | bytes 65568 | tf_op jit(solution)/shard_map/ppermute | solution.py:18
  39.9 2.8 %collective-permute-done.6 = bf16[32,1,8,128]{3,0,2,1:T(8,128)(2,1)S(1)} collective-permute-done((bf16[32,1,8,128]{3,0,2,1:T(8,128)(2,1)S(1)}, bf16[32,1,8,128]{3,0,2,1:T(8,128)(2,1)S(1)}, u32[]{:S(2)}, u32[]{:S(2)}) %collective-permute-start.6) | collective-permute-done | bytes 65568 | tf_op jit(solution)/shard_map/ppermute | solution.py:15
  64.6 1.2 collective-permute-start.15
  65.8 0.9 collective-permute-start.20
  67.0 10.6 %collective-permute-done.15 = f32[3,3,3,32,32]{4,3,2,1,0:T(8,128)S(1)} collective-permute-done((f32[3,3,3,32,32]{4,3,2,1,0:T(8,128)S(1)}, f32[3,3,3,32,32]{4,3,2,1,0:T(8,128)S(1)}, u32[]{:S(2)}, u32[]{:S(2)}) %collective-permute-start.15) | collective-permute-done | bytes 110624 | tf_op jit(solution)/shard_map/ppermute | solution.py:32
  77.7 1.9 %collective-permute-done.20 = f32[217,128]{1,0:T(8,128)S(1)} collective-permute-done((f32[217,128]{1,0:T(8,128)S(1)}, f32[217,128]{1,0:T(8,128)S(1)}, u32[]{:S(2)}, u32[]{:S(2)}) %collective-permute-start.20) | collective-permute-done | bytes 111136 | tf_op jit(solution)/shard_map/ppermute | solution.py:32
  80.1 10.2 %collective-permute-done.16 = f32[3,3,3,32,32]{4,3,2,1,0:T(8,128)S(1)} collective-permute-done((f32[3,3,3,32,32]{4,3,2,1,0:T(8,128)S(1)}, f32[3,3,3,32,32]{4,3,2,1,0:T(8,128)S(1)}, u32[]{:S(2)}, u32[]{:S(2)}) %collective-permute-start.16) | collective-permute-done | bytes 110624 | tf_op jit(solution)/shard_map/ppermute | solution.py:32
  90.4 1.1 collective-permute-done.21
  91.5 1.0 collective-permute-start.22
  92.8 8.2 %collective-permute-done.17 = f32[3,3,3,32,32]{4,3,2,1,0:T(8,128)S(1)} collective-permute-done((f32[3,3,3,32,32]{4,3,2,1,0:T(8,128)S(1)}, f32[3,3,3,32,32]{4,3,2,1,0:T(8,128)S(1)}, u32[]{:S(2)}, u32[]{:S(2)}) %collective-permute-start.17) | collective-permute-done | bytes 110624 | tf_op jit(solution)/shard_map/ppermute | solution.py:32
  101.1 2.2 %collective-permute-done.22 = f32[217,128]{1,0:T(8,128)S(1)} collective-permute-done((f32[217,128]{1,0:T(8,128)S(1)}, f32[217,128]{1,0:T(8,128)S(1)}, u32[]{:S(2)}, u32[]{:S(2)}) %collective-permute-start.22) | collective-permute-done | bytes 111136 | tf_op jit(solution)/shard_map/ppermute | solution.py:32
  105.0 16.0 %collective-permute-done.18 = f32[3,3,3,32,32]{4,3,2,1,0:T(8,128)S(1)} collective-permute-done((f32[3,3,3,32,32]{4,3,2,1,0:T(8,128)S(1)}, f32[3,3,3,32,32]{4,3,2,1,0:T(8,128)S(1)}, u32[]{:S(2)}, u32[]{:S(2)}) %collective-permute-start.18) | collective-permute-done | bytes 110624 | tf_op jit(solution)/shard_map/ppermute | solution.py:32
  121.8 1.5 %collective-permute-done.23 = f32[217,128]{1,0:T(8,128)S(1)} collective-permute-done((f32[217,128]{1,0:T(8,128)S(1)}, f32[217,128]{1,0:T(8,128)S(1)}, u32[]{:S(2)}, u32[]{:S(2)}) %collective-permute-start.23) | collective-permute-done | bytes 111136 | tf_op jit(solution)/shard_map/ppermute | solution.py:32
  (203 shorter events, 38.4 us)
Async XLA Ops:
  2.6 2.4 %collective-permute-start = (f32[2,2,128]{2,1,0:T(2,128)S(1)}, f32[2,2,128]{2,1,0:T(2,128)S(1)}, u32[]{:S(2)}, u32[]{:S(2)}) collective-permute-start(f32[2,2,128]{2,1,0:T(2,128)S(1)} %pad_maximum_fusion.28), channel_id=1, source_target_pairs={{0,1},{1,0},{2,3},{3,2},{4,5},{5,4},{6,7},{7,6},{8,9},{9,8},{10,11... | collective-permute-start | bytes 6152 | tf_op jit(solution)/shard_map/ppermute | solution.py:32
  5.1 7.2 %collective-permute-start.1 = (f32[2,2,128]{2,1,0:T(2,128)S(1)}, f32[2,2,128]{2,1,0:T(2,128)S(1)}, u32[]{:S(2)}, u32[]{:S(2)}) collective-permute-start(f32[2,2,128]{2,1,0:T(2,128)S(1)} %fusion.352), channel_id=1, source_target_pairs={{0,2},{1,3},{2,0},{3,1},{4,6},{5,7},{6,4},{7,5},{8,10},{9,11},{10,... | collective-permute-start | bytes 6152 | tf_op jit(solution)/shard_map/ppermute | solution.py:32
  7.7 30.0 %collective-permute-start.11 = (bf16[2,32,1,8,128]{4,1,3,2,0:T(8,128)(2,1)S(1)}, bf16[2,32,1,8,128]{4,1,3,2,0:T(8,128)(2,1)S(1)}, u32[]{:S(2)}, u32[]{:S(2)}) collective-permute-start(bf16[2,32,1,8,128]{4,1,3,2,0:T(8,128)(2,1)S(1)} %get-tuple-element.37), channel_id=1, source_target_pairs={{4,0},{8,4},{12,8},{16,12},{20,16},{24,20},{28,24},{0,28},{5,1},{9... | collective-permute-start | bytes 393224 | tf_op jit(solution)/shard_map/ppermute | solution.py:18
  12.3 25.4 %collective-permute-start.10 = (bf16[2,32,1,8,128]{4,1,3,2,0:T(8,128)(2,1)S(1)}, bf16[2,32,1,8,128]{4,1,3,2,0:T(8,128)(2,1)S(1)}, u32[]{:S(2)}, u32[]{:S(2)}) collective-permute-start(bf16[2,32,1,8,128]{4,1,3,2,0:T(8,128)(2,1)S(1)} %get-tuple-element.36), channel_id=1, source_target_pairs={{0,4},{4,8},{8,12},{12,16},{16,20},{20,24},{24,28},{28,0},{1,5},{5... | collective-permute-start | bytes 393224 | tf_op jit(solution)/shard_map/ppermute | solution.py:15
  12.7 6.7 %collective-permute-start.3 = (bf16[32,1,8,128]{3,0,2,1:T(8,128)(2,1)S(1)}, bf16[32,1,8,128]{3,0,2,1:T(8,128)(2,1)S(1)}, u32[]{:S(2)}, u32[]{:S(2)}) collective-permute-start(bf16[32,1,8,128]{3,0,2,1:T(8,128)(2,1)S(1)} %get-tuple-element.49), channel_id=1, source_target_pairs={{4,0},{8,4},{12,8},{16,12},{20,16},{24,20},{28,24},{0,28},{5,1},{9... | collective-permute-start | bytes 196616 | tf_op jit(solution)/shard_map/ppermute | solution.py:18
  17.5 7.0 %collective-permute-start.2 = (bf16[32,1,8,128]{3,0,2,1:T(8,128)(2,1)S(1)}, bf16[32,1,8,128]{3,0,2,1:T(8,128)(2,1)S(1)}, u32[]{:S(2)}, u32[]{:S(2)}) collective-permute-start(bf16[32,1,8,128]{3,0,2,1:T(8,128)(2,1)S(1)} %get-tuple-element.48), channel_id=1, source_target_pairs={{0,4},{4,8},{8,12},{12,16},{16,20},{20,24},{24,28},{28,0},{1,5},{5... | collective-permute-start | bytes 196616 | tf_op jit(solution)/shard_map/ppermute | solution.py:15
  24.5 1.8 %collective-permute-start.5 = (bf16[32,4,1,128]{3,0,2,1:T(8,128)(2,1)S(1)}, bf16[32,4,1,128]{3,0,2,1:T(8,128)(2,1)S(1)}, u32[]{:S(2)}, u32[]{:S(2)}) collective-permute-start(bf16[32,4,1,128]{3,0,2,1:T(8,128)(2,1)S(1)} %get-tuple-element.45), channel_id=1, source_target_pairs={{1,0},{2,1},{3,2},{0,3},{5,4},{6,5},{7,6},{4,7},{9,8},{10,9},{11,1... | collective-permute-start | bytes 98312 | tf_op jit(solution)/shard_map/ppermute | solution.py:18
  24.5 3.4 %collective-permute-start.4 = (bf16[32,4,1,128]{3,0,2,1:T(8,128)(2,1)S(1)}, bf16[32,4,1,128]{3,0,2,1:T(8,128)(2,1)S(1)}, u32[]{:S(2)}, u32[]{:S(2)}) collective-permute-start(bf16[32,4,1,128]{3,0,2,1:T(8,128)(2,1)S(1)} %get-tuple-element.44), channel_id=1, source_target_pairs={{0,1},{1,2},{2,3},{3,0},{4,5},{5,6},{6,7},{7,4},{8,9},{9,10},{10,1... | collective-permute-start | bytes 98312 | tf_op jit(solution)/shard_map/ppermute | solution.py:15
  35.6 4.3 %collective-permute-start.7 = (bf16[32,1,8,128]{3,0,2,1:T(8,128)(2,1)S(1)}, bf16[32,1,8,128]{3,0,2,1:T(8,128)(2,1)S(1)}, u32[]{:S(2)}, u32[]{:S(2)}) collective-permute-start(bf16[32,1,8,128]{3,0,2,1:T(8,128)(2,1)S(1)} %get-tuple-element.47), channel_id=1, source_target_pairs={{4,0},{8,4},{12,8},{16,12},{20,16},{24,20},{28,24},{0,28},{5,1},{9... | collective-permute-start | bytes 196616 | tf_op jit(solution)/shard_map/ppermute | solution.py:18
  35.6 7.0 %collective-permute-start.6 = (bf16[32,1,8,128]{3,0,2,1:T(8,128)(2,1)S(1)}, bf16[32,1,8,128]{3,0,2,1:T(8,128)(2,1)S(1)}, u32[]{:S(2)}, u32[]{:S(2)}) collective-permute-start(bf16[32,1,8,128]{3,0,2,1:T(8,128)(2,1)S(1)} %get-tuple-element.46), channel_id=1, source_target_pairs={{0,4},{4,8},{8,12},{12,16},{16,20},{20,24},{24,28},{28,0},{1,5},{5... | collective-permute-start | bytes 196616 | tf_op jit(solution)/shard_map/ppermute | solution.py:15
  37.7 5.6 %collective-permute-start.13 = (bf16[2,32,4,1,128]{4,1,3,2,0:T(8,128)(2,1)S(1)}, bf16[2,32,4,1,128]{4,1,3,2,0:T(8,128)(2,1)S(1)}, u32[]{:S(2)}, u32[]{:S(2)}) collective-permute-start(bf16[2,32,4,1,128]{4,1,3,2,0:T(8,128)(2,1)S(1)} %get-tuple-element.27), channel_id=1, source_target_pairs={{1,0},{2,1},{3,2},{0,3},{5,4},{6,5},{7,6},{4,7},{9,8},{10,9},{11,1... | collective-permute-start | bytes 196616 | tf_op jit(solution)/shard_map/ppermute | solution.py:18
  37.7 5.5 %collective-permute-start.12 = (bf16[2,32,4,1,128]{4,1,3,2,0:T(8,128)(2,1)S(1)}, bf16[2,32,4,1,128]{4,1,3,2,0:T(8,128)(2,1)S(1)}, u32[]{:S(2)}, u32[]{:S(2)}) collective-permute-start(bf16[2,32,4,1,128]{4,1,3,2,0:T(8,128)(2,1)S(1)} %get-tuple-element.26), channel_id=1, source_target_pairs={{0,1},{1,2},{2,3},{3,0},{4,5},{5,6},{6,7},{7,4},{8,9},{9,10},{10,1... | collective-permute-start | bytes 196616 | tf_op jit(solution)/shard_map/ppermute | solution.py:15
  42.7 15.3 %collective-permute-start.9 = (bf16[32,4,1,128]{3,0,2,1:T(8,128)(2,1)S(1)}, bf16[32,4,1,128]{3,0,2,1:T(8,128)(2,1)S(1)}, u32[]{:S(2)}, u32[]{:S(2)}) collective-permute-start(bf16[32,4,1,128]{3,0,2,1:T(8,128)(2,1)S(1)} %get-tuple-element.41), channel_id=1, source_target_pairs={{1,0},{2,1},{3,2},{0,3},{5,4},{6,5},{7,6},{4,7},{9,8},{10,9},{11,1... | collective-permute-start | bytes 98312 | tf_op jit(solution)/shard_map/ppermute | solution.py:18
  42.7 15.2 %collective-permute-start.8 = (bf16[32,4,1,128]{3,0,2,1:T(8,128)(2,1)S(1)}, bf16[32,4,1,128]{3,0,2,1:T(8,128)(2,1)S(1)}, u32[]{:S(2)}, u32[]{:S(2)}) collective-permute-start(bf16[32,4,1,128]{3,0,2,1:T(8,128)(2,1)S(1)} %get-tuple-element.40), channel_id=1, source_target_pairs={{0,1},{1,2},{2,3},{3,0},{4,5},{5,6},{6,7},{7,4},{8,9},{9,10},{10,1... | collective-permute-start | bytes 98312 | tf_op jit(solution)/shard_map/ppermute | solution.py:15
  50.8 13.7 %collective-permute-start.14 = (f32[3,3,3,32,32]{4,3,2,1,0:T(8,128)S(1)}, f32[3,3,3,32,32]{4,3,2,1,0:T(8,128)S(1)}, u32[]{:S(2)}, u32[]{:S(2)}) collective-permute-start(f32[3,3,3,32,32]{4,3,2,1,0:T(8,128)S(1)} %bitcast.1110), channel_id=1, source_target_pairs={{0,1},{1,0},{2,3},{3,2},{4,5},{5,4},{6,7},{7,6},{8,9},{9,8},{10,11... | collective-permute-start | bytes 331784 | tf_op jit(solution)/shard_map/ppermute | solution.py:32
  57.9 7.9 %collective-permute-start.19 = (f32[217,128]{1,0:T(8,128)S(1)}, f32[217,128]{1,0:T(8,128)S(1)}, u32[]{:S(2)}, u32[]{:S(2)}) collective-permute-start(f32[217,128]{1,0:T(8,128)S(1)} %pad_bitcast_fusion), channel_id=1, source_target_pairs={{0,1},{1,0},{2,3},{3,2},{4,5},{5,4},{6,7},{7,6},{8,9},{9,8},{10,11... | collective-permute-start | bytes 333320 | tf_op jit(solution)/shard_map/ppermute | solution.py:32
  64.6 13.0 %collective-permute-start.15 = (f32[3,3,3,32,32]{4,3,2,1,0:T(8,128)S(1)}, f32[3,3,3,32,32]{4,3,2,1,0:T(8,128)S(1)}, u32[]{:S(2)}, u32[]{:S(2)}) collective-permute-start(f32[3,3,3,32,32]{4,3,2,1,0:T(8,128)S(1)} %add.321), channel_id=1, source_target_pairs={{0,2},{1,3},{2,0},{3,1},{4,6},{5,7},{6,4},{7,5},{8,10},{9,11},{10,... | collective-permute-start | bytes 331784 | tf_op jit(solution)/shard_map/ppermute | solution.py:32
  65.8 13.8 %collective-permute-start.20 = (f32[217,128]{1,0:T(8,128)S(1)}, f32[217,128]{1,0:T(8,128)S(1)}, u32[]{:S(2)}, u32[]{:S(2)}) collective-permute-start(f32[217,128]{1,0:T(8,128)S(1)} %fusion.353), channel_id=1, source_target_pairs={{0,2},{1,3},{2,0},{3,1},{4,6},{5,7},{6,4},{7,5},{8,10},{9,11},{10,... | collective-permute-start | bytes 333320 | tf_op jit(solution)/shard_map/ppermute | solution.py:32
  77.7 12.6 %collective-permute-start.16 = (f32[3,3,3,32,32]{4,3,2,1,0:T(8,128)S(1)}, f32[3,3,3,32,32]{4,3,2,1,0:T(8,128)S(1)}, u32[]{:S(2)}, u32[]{:S(2)}) collective-permute-start(f32[3,3,3,32,32]{4,3,2,1,0:T(8,128)S(1)} %add.322), channel_id=1, source_target_pairs={{0,4},{4,0},{8,12},{12,8},{16,20},{20,16},{24,28},{28,24},{1,5},{5... | collective-permute-start | bytes 331784 | tf_op jit(solution)/shard_map/ppermute | solution.py:32
  79.7 11.9 %collective-permute-start.21 = (f32[217,128]{1,0:T(8,128)S(1)}, f32[217,128]{1,0:T(8,128)S(1)}, u32[]{:S(2)}, u32[]{:S(2)}) collective-permute-start(f32[217,128]{1,0:T(8,128)S(1)} %fusion.417), channel_id=1, source_target_pairs={{0,4},{4,0},{8,12},{12,8},{16,20},{20,16},{24,28},{28,24},{1,5},{5... | collective-permute-start | bytes 333320 | tf_op jit(solution)/shard_map/ppermute | solution.py:32
  90.4 10.6 %collective-permute-start.17 = (f32[3,3,3,32,32]{4,3,2,1,0:T(8,128)S(1)}, f32[3,3,3,32,32]{4,3,2,1,0:T(8,128)S(1)}, u32[]{:S(2)}, u32[]{:S(2)}) collective-permute-start(f32[3,3,3,32,32]{4,3,2,1,0:T(8,128)S(1)} %add.323), channel_id=1, source_target_pairs={{0,8},{4,12},{8,0},{12,4},{16,24},{20,28},{24,16},{28,20},{1,9},{5... | collective-permute-start | bytes 331784 | tf_op jit(solution)/shard_map/ppermute | solution.py:32
  91.5 11.8 %collective-permute-start.22 = (f32[217,128]{1,0:T(8,128)S(1)}, f32[217,128]{1,0:T(8,128)S(1)}, u32[]{:S(2)}, u32[]{:S(2)}) collective-permute-start(f32[217,128]{1,0:T(8,128)S(1)} %add.329), channel_id=1, source_target_pairs={{0,8},{4,12},{8,0},{12,4},{16,24},{20,28},{24,16},{28,20},{1,9},{5... | collective-permute-start | bytes 333320 | tf_op jit(solution)/shard_map/ppermute | solution.py:32
  101.0 20.0 %collective-permute-start.18 = (f32[3,3,3,32,32]{4,3,2,1,0:T(8,128)S(1)}, f32[3,3,3,32,32]{4,3,2,1,0:T(8,128)S(1)}, u32[]{:S(2)}, u32[]{:S(2)}) collective-permute-start(f32[3,3,3,32,32]{4,3,2,1,0:T(8,128)S(1)} %add.324), channel_id=1, source_target_pairs={{0,16},{4,20},{8,24},{12,28},{16,0},{20,4},{24,8},{28,12},{1,17},{... | collective-permute-start | bytes 331784 | tf_op jit(solution)/shard_map/ppermute | solution.py:32
  103.4 20.0 %collective-permute-start.23 = (f32[217,128]{1,0:T(8,128)S(1)}, f32[217,128]{1,0:T(8,128)S(1)}, u32[]{:S(2)}, u32[]{:S(2)}) collective-permute-start(f32[217,128]{1,0:T(8,128)S(1)} %add.330), channel_id=1, source_target_pairs={{0,16},{4,20},{8,24},{12,28},{16,0},{20,4},{24,8},{28,12},{1,17},{... | collective-permute-start | bytes 333320 | tf_op jit(solution)/shard_map/ppermute | solution.py:32
  (7 other events, 39.0 us)

commit v2 on v1

--- a/solution.py
+++ b/solution.py
@@ -153,7 +153,9 @@
     grad_second, grad_out, grad_bias = unpack_rows(
         butterfly_sum(pack_rows(early), ("los", "sky")), early_shapes
     )
-    grad_first = butterfly_sum(grad_first * norm_factor, ("los", "sky"))
+    (grad_first,) = unpack_rows(
+        butterfly_sum(pack_rows((grad_first * norm_factor,)), ("los", "sky")), [grad_first.shape]
+    )
     return (grad_features, grad_first, grad_second, grad_out, grad_bias)
 
 

time: 126 us -> 95.8 us (0.76)
  waiting for transfers between devices: 65.8 us -> 35.8 us
    ppermute x12, waiting for transfers between devices: 51.8 us -> 21.8 us  [butterfly_sum(): value = value + lax.ppermute(value, axis, pairs)]
  transfers between devices with their start and end apart: 24 -> 24, of which waited for: 14 -> 14; matrix products, arithmetic and copies ran while one was open for 25% -> 33% of each run, Pallas kernels for 0% -> 0%
where the time goes in v2:
time: 95.8 us; the launch traced here: 95.6 us
  waiting for transfers between devices  35.8 us (37%)
  matrix products  24.3 us (25%)
  starting transfers between devices  21.2 us (22%)
  local copies, waits for them, and re-layouts  7.99 us (8%)
  other arithmetic  4.76 us (5%)
  between operations  1.47 us (2%)
    ppermute x12, waiting for transfers between devices, butterfly_sum(): value = value + lax.ppermute(value, axis, pairs)  21.8 us
    dot_general x54, matrix products, spread_local(): jnp.einsum('oi,oxzy->ixzy', weight[tap_x, tap_z, tap_y], window, preferre...  12 us
    dot_general x54, matrix products, taps_from_inputs(): jnp.einsum('oxzy,ixzy->oi', grad_field, window, preferred_element_type=jn...  11.8 us
    ppermute x6, starting transfers between devices, extended(): lax.ppermute(lax.slice_in_dim(block, 0, width, axis=dim), axis, backward)  9.61 us
    ppermute x6, waiting for transfers between devices, extended(): lax.ppermute(lax.slice_in_dim(block, block.shape[dim] - width, None, axis...  9.45 us
    ppermute x12, starting transfers between devices, butterfly_sum(): value = value + lax.ppermute(value, axis, pairs)  8.1 us
    ppermute x6, waiting for transfers between devices, extended(): lax.ppermute(lax.slice_in_dim(block, 0, width, axis=dim), axis, backward)  4.6 us
    unnamed x17, local copies, waits for them, and re-layouts  3.7 us
  transfers between devices with their start and end apart: 24, of which 14 were waited for; matrix products, arithmetic and copies ran while one was open for 33% of the time, Pallas kernels for 0%

profile of v2, /device:TPU:0, one launch (start us, length us, event | category | flops | bytes accessed | tf_op | source)
XLA Modules:
  0.0 95.6 jit_solution(6847753845377315136)
XLA Ops:
  0.7 1.0 %fusion.100 = bf16[32,2,8,128]{3,0,2,1:T(8,128)(2,1)S(1)} fusion(bf16[32,2,8,128]{3,2,1,0:T(8,128)(2,1)} %param.11), kind=kLoop, calls=%fused_computation.223 | loop fusion | flops 393216 | bytes 262144 | tf_op jit(solution)/shard_map/convert_element_type | solution.py:111
  3.2 0.9 copy.370
  4.1 0.9 copy.371
  5.1 2.6 %collective-permute-start.1 = (f32[2,2,128]{2,1,0:T(2,128)S(1)}, f32[2,2,128]{2,1,0:T(2,128)S(1)}, u32[]{:S(2)}, u32[]{:S(2)}) collective-permute-start(f32[2,2,128]{2,1,0:T(2,128)S(1)} %fusion.352), channel_id=1, source_target_pairs={{0,2},{1,3},{2,0},{3,1},{4,6},{5,7},{6,4},{7,5},{8,10},{9,11},{10,... | collective-permute-start | bytes 6152 | tf_op jit(solution)/shard_map/ppermute | solution.py:32
  7.7 4.6 %collective-permute-start.11 = (bf16[2,32,1,8,128]{4,1,3,2,0:T(8,128)(2,1)S(1)}, bf16[2,32,1,8,128]{4,1,3,2,0:T(8,128)(2,1)S(1)}, u32[]{:S(2)}, u32[]{:S(2)}) collective-permute-start(bf16[2,32,1,8,128]{4,1,3,2,0:T(8,128)(2,1)S(1)} %get-tuple-element.37), channel_id=1, source_target_pairs={{4,0},{8,4},{12,8},{16,12},{20,16},{24,20},{28,24},{0,28},{5,1},{9... | collective-permute-start | bytes 393224 | tf_op jit(solution)/shard_map/ppermute | solution.py:18
  12.7 4.8 %collective-permute-start.3 = (bf16[32,1,8,128]{3,0,2,1:T(8,128)(2,1)S(1)}, bf16[32,1,8,128]{3,0,2,1:T(8,128)(2,1)S(1)}, u32[]{:S(2)}, u32[]{:S(2)}) collective-permute-start(bf16[32,1,8,128]{3,0,2,1:T(8,128)(2,1)S(1)} %get-tuple-element.49), channel_id=1, source_target_pairs={{4,0},{8,4},{12,8},{16,12},{20,16},{24,20},{28,24},{0,28},{5,1},{9... | collective-permute-start | bytes 196616 | tf_op jit(solution)/shard_map/ppermute | solution.py:18
  17.6 1.8 %collective-permute-done.3 = bf16[32,1,8,128]{3,0,2,1:T(8,128)(2,1)S(1)} collective-permute-done((bf16[32,1,8,128]{3,0,2,1:T(8,128)(2,1)S(1)}, bf16[32,1,8,128]{3,0,2,1:T(8,128)(2,1)S(1)}, u32[]{:S(2)}, u32[]{:S(2)}) %collective-permute-start.3) | collective-permute-done | bytes 65568 | tf_op jit(solution)/shard_map/ppermute | solution.py:18
  19.4 5.1 %collective-permute-done.2 = bf16[32,1,8,128]{3,0,2,1:T(8,128)(2,1)S(1)} collective-permute-done((bf16[32,1,8,128]{3,0,2,1:T(8,128)(2,1)S(1)}, bf16[32,1,8,128]{3,0,2,1:T(8,128)(2,1)S(1)}, u32[]{:S(2)}, u32[]{:S(2)}) %collective-permute-start.2) | collective-permute-done | bytes 65568 | tf_op jit(solution)/shard_map/ppermute | solution.py:15
  25.1 1.2 %collective-permute-done.5 = bf16[32,4,1,128]{3,0,2,1:T(8,128)(2,1)S(1)} collective-permute-done((bf16[32,4,1,128]{3,0,2,1:T(8,128)(2,1)S(1)}, bf16[32,4,1,128]{3,0,2,1:T(8,128)(2,1)S(1)}, u32[]{:S(2)}, u32[]{:S(2)}) %collective-permute-start.5) | collective-permute-done | bytes 32800 | tf_op jit(solution)/shard_map/ppermute | solution.py:18
  26.3 1.6 %collective-permute-done.4 = bf16[32,4,1,128]{3,0,2,1:T(8,128)(2,1)S(1)} collective-permute-done((bf16[32,4,1,128]{3,0,2,1:T(8,128)(2,1)S(1)}, bf16[32,4,1,128]{3,0,2,1:T(8,128)(2,1)S(1)}, u32[]{:S(2)}, u32[]{:S(2)}) %collective-permute-start.4) | collective-permute-done | bytes 32800 | tf_op jit(solution)/shard_map/ppermute | solution.py:15
  35.6 2.0 %collective-permute-start.6 = (bf16[32,1,8,128]{3,0,2,1:T(8,128)(2,1)S(1)}, bf16[32,1,8,128]{3,0,2,1:T(8,128)(2,1)S(1)}, u32[]{:S(2)}, u32[]{:S(2)}) collective-permute-start(bf16[32,1,8,128]{3,0,2,1:T(8,128)(2,1)S(1)} %get-tuple-element.46), channel_id=1, source_target_pairs={{0,4},{4,8},{8,12},{12,16},{16,20},{20,24},{24,28},{28,0},{1,5},{5... | collective-permute-start | bytes 196616 | tf_op jit(solution)/shard_map/ppermute | solution.py:15
  38.2 1.7 %collective-permute-done.7 = bf16[32,1,8,128]{3,0,2,1:T(8,128)(2,1)S(1)} collective-permute-done((bf16[32,1,8,128]{3,0,2,1:T(8,128)(2,1)S(1)}, bf16[32,1,8,128]{3,0,2,1:T(8,128)(2,1)S(1)}, u32[]{:S(2)}, u32[]{:S(2)}) %collective-permute-start.7) | collective-permute-done | bytes 65568 | tf_op jit(solution)/shard_map/ppermute | solution.py:18
  39.9 2.8 %collective-permute-done.6 = bf16[32,1,8,128]{3,0,2,1:T(8,128)(2,1)S(1)} collective-permute-done((bf16[32,1,8,128]{3,0,2,1:T(8,128)(2,1)S(1)}, bf16[32,1,8,128]{3,0,2,1:T(8,128)(2,1)S(1)}, u32[]{:S(2)}, u32[]{:S(2)}) %collective-permute-start.6) | collective-permute-done | bytes 65568 | tf_op jit(solution)/shard_map/ppermute | solution.py:15
  64.7 1.2 %collective-permute-start.15 = (f32[216,128]{1,0:T(8,128)S(1)}, f32[216,128]{1,0:T(8,128)S(1)}, u32[]{:S(2)}, u32[]{:S(2)}) collective-permute-start(f32[216,128]{1,0:T(8,128)S(1)} %add.321), channel_id=1, source_target_pairs={{0,2},{1,3},{2,0},{3,1},{4,6},{5,7},{6,4},{7,5},{8,10},{9,11},{10,... | collective-permute-start | bytes 331784 | tf_op jit(solution)/shard_map/ppermute | solution.py:32
  65.9 0.9 collective-permute-start.20
  67.1 3.5 %collective-permute-done.15 = f32[216,128]{1,0:T(8,128)S(1)} collective-permute-done((f32[216,128]{1,0:T(8,128)S(1)}, f32[216,128]{1,0:T(8,128)S(1)}, u32[]{:S(2)}, u32[]{:S(2)}) %collective-permute-start.15) | collective-permute-done | bytes 110624 | tf_op jit(solution)/shard_map/ppermute | solution.py:32
  70.7 1.9 %collective-permute-done.20 = f32[217,128]{1,0:T(8,128)S(1)} collective-permute-done((f32[217,128]{1,0:T(8,128)S(1)}, f32[217,128]{1,0:T(8,128)S(1)}, u32[]{:S(2)}, u32[]{:S(2)}) %collective-permute-start.20) | collective-permute-done | bytes 111136 | tf_op jit(solution)/shard_map/ppermute | solution.py:32
  73.1 2.8 %collective-permute-done.16 = f32[216,128]{1,0:T(8,128)S(1)} collective-permute-done((f32[216,128]{1,0:T(8,128)S(1)}, f32[216,128]{1,0:T(8,128)S(1)}, u32[]{:S(2)}, u32[]{:S(2)}) %collective-permute-start.16) | collective-permute-done | bytes 110624 | tf_op jit(solution)/shard_map/ppermute | solution.py:32
  76.0 1.9 %collective-permute-done.21 = f32[217,128]{1,0:T(8,128)S(1)} collective-permute-done((f32[217,128]{1,0:T(8,128)S(1)}, f32[217,128]{1,0:T(8,128)S(1)}, u32[]{:S(2)}, u32[]{:S(2)}) %collective-permute-start.21) | collective-permute-done | bytes 111136 | tf_op jit(solution)/shard_map/ppermute | solution.py:32
  78.3 4.5 %collective-permute-done.17 = f32[216,128]{1,0:T(8,128)S(1)} collective-permute-done((f32[216,128]{1,0:T(8,128)S(1)}, f32[216,128]{1,0:T(8,128)S(1)}, u32[]{:S(2)}, u32[]{:S(2)}) %collective-permute-start.17) | collective-permute-done | bytes 110624 | tf_op jit(solution)/shard_map/ppermute | solution.py:32
  82.8 1.5 %collective-permute-done.22 = f32[217,128]{1,0:T(8,128)S(1)} collective-permute-done((f32[217,128]{1,0:T(8,128)S(1)}, f32[217,128]{1,0:T(8,128)S(1)}, u32[]{:S(2)}, u32[]{:S(2)}) %collective-permute-start.22) | collective-permute-done | bytes 111136 | tf_op jit(solution)/shard_map/ppermute | solution.py:32
  84.4 1.5 %collective-permute-start.23 = (f32[217,128]{1,0:T(8,128)S(1)}, f32[217,128]{1,0:T(8,128)S(1)}, u32[]{:S(2)}, u32[]{:S(2)}) collective-permute-start(f32[217,128]{1,0:T(8,128)S(1)} %add.330), channel_id=1, source_target_pairs={{0,16},{4,20},{8,24},{12,28},{16,0},{20,4},{24,8},{28,12},{1,17},{... | collective-permute-start | bytes 333320 | tf_op jit(solution)/shard_map/ppermute | solution.py:32
  86.8 5.3 %collective-permute-done.18 = f32[216,128]{1,0:T(8,128)S(1)} collective-permute-done((f32[216,128]{1,0:T(8,128)S(1)}, f32[216,128]{1,0:T(8,128)S(1)}, u32[]{:S(2)}, u32[]{:S(2)}) %collective-permute-start.18) | collective-permute-done | bytes 110624 | tf_op jit(solution)/shard_map/ppermute | solution.py:32
  92.1 0.9 reshape_reshape.3
  (205 shorter events, 37.2 us)
Async XLA Ops:
  2.6 2.4 %collective-permute-start = (f32[2,2,128]{2,1,0:T(2,128)S(1)}, f32[2,2,128]{2,1,0:T(2,128)S(1)}, u32[]{:S(2)}, u32[]{:S(2)}) collective-permute-start(f32[2,2,128]{2,1,0:T(2,128)S(1)} %pad_maximum_fusion.28), channel_id=1, source_target_pairs={{0,1},{1,0},{2,3},{3,2},{4,5},{5,4},{6,7},{7,6},{8,9},{9,8},{10,11... | collective-permute-start | bytes 6152 | tf_op jit(solution)/shard_map/ppermute | solution.py:32
  5.1 7.2 %collective-permute-start.1 = (f32[2,2,128]{2,1,0:T(2,128)S(1)}, f32[2,2,128]{2,1,0:T(2,128)S(1)}, u32[]{:S(2)}, u32[]{:S(2)}) collective-permute-start(f32[2,2,128]{2,1,0:T(2,128)S(1)} %fusion.352), channel_id=1, source_target_pairs={{0,2},{1,3},{2,0},{3,1},{4,6},{5,7},{6,4},{7,5},{8,10},{9,11},{10,... | collective-permute-start | bytes 6152 | tf_op jit(solution)/shard_map/ppermute | solution.py:32
  7.7 30.0 %collective-permute-start.11 = (bf16[2,32,1,8,128]{4,1,3,2,0:T(8,128)(2,1)S(1)}, bf16[2,32,1,8,128]{4,1,3,2,0:T(8,128)(2,1)S(1)}, u32[]{:S(2)}, u32[]{:S(2)}) collective-permute-start(bf16[2,32,1,8,128]{4,1,3,2,0:T(8,128)(2,1)S(1)} %get-tuple-element.37), channel_id=1, source_target_pairs={{4,0},{8,4},{12,8},{16,12},{20,16},{24,20},{28,24},{0,28},{5,1},{9... | collective-permute-start | bytes 393224 | tf_op jit(solution)/shard_map/ppermute | solution.py:18
  12.3 25.4 %collective-permute-start.10 = (bf16[2,32,1,8,128]{4,1,3,2,0:T(8,128)(2,1)S(1)}, bf16[2,32,1,8,128]{4,1,3,2,0:T(8,128)(2,1)S(1)}, u32[]{:S(2)}, u32[]{:S(2)}) collective-permute-start(bf16[2,32,1,8,128]{4,1,3,2,0:T(8,128)(2,1)S(1)} %get-tuple-element.36), channel_id=1, source_target_pairs={{0,4},{4,8},{8,12},{12,16},{16,20},{20,24},{24,28},{28,0},{1,5},{5... | collective-permute-start | bytes 393224 | tf_op jit(solution)/shard_map/ppermute | solution.py:15
  12.7 6.7 %collective-permute-start.3 = (bf16[32,1,8,128]{3,0,2,1:T(8,128)(2,1)S(1)}, bf16[32,1,8,128]{3,0,2,1:T(8,128)(2,1)S(1)}, u32[]{:S(2)}, u32[]{:S(2)}) collective-permute-start(bf16[32,1,8,128]{3,0,2,1:T(8,128)(2,1)S(1)} %get-tuple-element.49), channel_id=1, source_target_pairs={{4,0},{8,4},{12,8},{16,12},{20,16},{24,20},{28,24},{0,28},{5,1},{9... | collective-permute-start | bytes 196616 | tf_op jit(solution)/shard_map/ppermute | solution.py:18
  17.5 7.0 %collective-permute-start.2 = (bf16[32,1,8,128]{3,0,2,1:T(8,128)(2,1)S(1)}, bf16[32,1,8,128]{3,0,2,1:T(8,128)(2,1)S(1)}, u32[]{:S(2)}, u32[]{:S(2)}) collective-permute-start(bf16[32,1,8,128]{3,0,2,1:T(8,128)(2,1)S(1)} %get-tuple-element.48), channel_id=1, source_target_pairs={{0,4},{4,8},{8,12},{12,16},{16,20},{20,24},{24,28},{28,0},{1,5},{5... | collective-permute-start | bytes 196616 | tf_op jit(solution)/shard_map/ppermute | solution.py:15
  24.5 1.8 %collective-permute-start.5 = (bf16[32,4,1,128]{3,0,2,1:T(8,128)(2,1)S(1)}, bf16[32,4,1,128]{3,0,2,1:T(8,128)(2,1)S(1)}, u32[]{:S(2)}, u32[]{:S(2)}) collective-permute-start(bf16[32,4,1,128]{3,0,2,1:T(8,128)(2,1)S(1)} %get-tuple-element.45), channel_id=1, source_target_pairs={{1,0},{2,1},{3,2},{0,3},{5,4},{6,5},{7,6},{4,7},{9,8},{10,9},{11,1... | collective-permute-start | bytes 98312 | tf_op jit(solution)/shard_map/ppermute | solution.py:18
  24.5 3.4 %collective-permute-start.4 = (bf16[32,4,1,128]{3,0,2,1:T(8,128)(2,1)S(1)}, bf16[32,4,1,128]{3,0,2,1:T(8,128)(2,1)S(1)}, u32[]{:S(2)}, u32[]{:S(2)}) collective-permute-start(bf16[32,4,1,128]{3,0,2,1:T(8,128)(2,1)S(1)} %get-tuple-element.44), channel_id=1, source_target_pairs={{0,1},{1,2},{2,3},{3,0},{4,5},{5,6},{6,7},{7,4},{8,9},{9,10},{10,1... | collective-permute-start | bytes 98312 | tf_op jit(solution)/shard_map/ppermute | solution.py:15
  35.6 4.3 %collective-permute-start.7 = (bf16[32,1,8,128]{3,0,2,1:T(8,128)(2,1)S(1)}, bf16[32,1,8,128]{3,0,2,1:T(8,128)(2,1)S(1)}, u32[]{:S(2)}, u32[]{:S(2)}) collective-permute-start(bf16[32,1,8,128]{3,0,2,1:T(8,128)(2,1)S(1)} %get-tuple-element.47), channel_id=1, source_target_pairs={{4,0},{8,4},{12,8},{16,12},{20,16},{24,20},{28,24},{0,28},{5,1},{9... | collective-permute-start | bytes 196616 | tf_op jit(solution)/shard_map/ppermute | solution.py:18
  35.6 7.0 %collective-permute-start.6 = (bf16[32,1,8,128]{3,0,2,1:T(8,128)(2,1)S(1)}, bf16[32,1,8,128]{3,0,2,1:T(8,128)(2,1)S(1)}, u32[]{:S(2)}, u32[]{:S(2)}) collective-permute-start(bf16[32,1,8,128]{3,0,2,1:T(8,128)(2,1)S(1)} %get-tuple-element.46), channel_id=1, source_target_pairs={{0,4},{4,8},{8,12},{12,16},{16,20},{20,24},{24,28},{28,0},{1,5},{5... | collective-permute-start | bytes 196616 | tf_op jit(solution)/shard_map/ppermute | solution.py:15
  37.7 5.6 %collective-permute-start.13 = (bf16[2,32,4,1,128]{4,1,3,2,0:T(8,128)(2,1)S(1)}, bf16[2,32,4,1,128]{4,1,3,2,0:T(8,128)(2,1)S(1)}, u32[]{:S(2)}, u32[]{:S(2)}) collective-permute-start(bf16[2,32,4,1,128]{4,1,3,2,0:T(8,128)(2,1)S(1)} %get-tuple-element.27), channel_id=1, source_target_pairs={{1,0},{2,1},{3,2},{0,3},{5,4},{6,5},{7,6},{4,7},{9,8},{10,9},{11,1... | collective-permute-start | bytes 196616 | tf_op jit(solution)/shard_map/ppermute | solution.py:18
  37.7 5.5 %collective-permute-start.12 = (bf16[2,32,4,1,128]{4,1,3,2,0:T(8,128)(2,1)S(1)}, bf16[2,32,4,1,128]{4,1,3,2,0:T(8,128)(2,1)S(1)}, u32[]{:S(2)}, u32[]{:S(2)}) collective-permute-start(bf16[2,32,4,1,128]{4,1,3,2,0:T(8,128)(2,1)S(1)} %get-tuple-element.26), channel_id=1, source_target_pairs={{0,1},{1,2},{2,3},{3,0},{4,5},{5,6},{6,7},{7,4},{8,9},{9,10},{10,1... | collective-permute-start | bytes 196616 | tf_op jit(solution)/shard_map/ppermute | solution.py:15
  42.7 15.4 %collective-permute-start.9 = (bf16[32,4,1,128]{3,0,2,1:T(8,128)(2,1)S(1)}, bf16[32,4,1,128]{3,0,2,1:T(8,128)(2,1)S(1)}, u32[]{:S(2)}, u32[]{:S(2)}) collective-permute-start(bf16[32,4,1,128]{3,0,2,1:T(8,128)(2,1)S(1)} %get-tuple-element.41), channel_id=1, source_target_pairs={{1,0},{2,1},{3,2},{0,3},{5,4},{6,5},{7,6},{4,7},{9,8},{10,9},{11,1... | collective-permute-start | bytes 98312 | tf_op jit(solution)/shard_map/ppermute | solution.py:18
  42.7 15.4 %collective-permute-start.8 = (bf16[32,4,1,128]{3,0,2,1:T(8,128)(2,1)S(1)}, bf16[32,4,1,128]{3,0,2,1:T(8,128)(2,1)S(1)}, u32[]{:S(2)}, u32[]{:S(2)}) collective-permute-start(bf16[32,4,1,128]{3,0,2,1:T(8,128)(2,1)S(1)} %get-tuple-element.40), channel_id=1, source_target_pairs={{0,1},{1,2},{2,3},{3,0},{4,5},{5,6},{6,7},{7,4},{8,9},{9,10},{10,1... | collective-permute-start | bytes 98312 | tf_op jit(solution)/shard_map/ppermute | solution.py:15
  51.0 13.6 %collective-permute-start.14 = (f32[216,128]{1,0:T(8,128)S(1)}, f32[216,128]{1,0:T(8,128)S(1)}, u32[]{:S(2)}, u32[]{:S(2)}) collective-permute-start(f32[216,128]{1,0:T(8,128)S(1)} %mul.96), channel_id=1, source_target_pairs={{0,1},{1,0},{2,3},{3,2},{4,5},{5,4},{6,7},{7,6},{8,9},{9,8},{10,11... | collective-permute-start | bytes 331784 | tf_op jit(solution)/shard_map/ppermute | solution.py:32
  58.0 7.9 %collective-permute-start.19 = (f32[217,128]{1,0:T(8,128)S(1)}, f32[217,128]{1,0:T(8,128)S(1)}, u32[]{:S(2)}, u32[]{:S(2)}) collective-permute-start(f32[217,128]{1,0:T(8,128)S(1)} %pad_bitcast_fusion), channel_id=1, source_target_pairs={{0,1},{1,0},{2,3},{3,2},{4,5},{5,4},{6,7},{7,6},{8,9},{9,8},{10,11... | collective-permute-start | bytes 333320 | tf_op jit(solution)/shard_map/ppermute | solution.py:32
  64.7 5.9 %collective-permute-start.15 = (f32[216,128]{1,0:T(8,128)S(1)}, f32[216,128]{1,0:T(8,128)S(1)}, u32[]{:S(2)}, u32[]{:S(2)}) collective-permute-start(f32[216,128]{1,0:T(8,128)S(1)} %add.321), channel_id=1, source_target_pairs={{0,2},{1,3},{2,0},{3,1},{4,6},{5,7},{6,4},{7,5},{8,10},{9,11},{10,... | collective-permute-start | bytes 331784 | tf_op jit(solution)/shard_map/ppermute | solution.py:32
  65.9 6.7 %collective-permute-start.20 = (f32[217,128]{1,0:T(8,128)S(1)}, f32[217,128]{1,0:T(8,128)S(1)}, u32[]{:S(2)}, u32[]{:S(2)}) collective-permute-start(f32[217,128]{1,0:T(8,128)S(1)} %fusion.353), channel_id=1, source_target_pairs={{0,2},{1,3},{2,0},{3,1},{4,6},{5,7},{6,4},{7,5},{8,10},{9,11},{10,... | collective-permute-start | bytes 333320 | tf_op jit(solution)/shard_map/ppermute | solution.py:32
  70.6 5.3 %collective-permute-start.16 = (f32[216,128]{1,0:T(8,128)S(1)}, f32[216,128]{1,0:T(8,128)S(1)}, u32[]{:S(2)}, u32[]{:S(2)}) collective-permute-start(f32[216,128]{1,0:T(8,128)S(1)} %add.322), channel_id=1, source_target_pairs={{0,4},{4,0},{8,12},{12,8},{16,20},{20,16},{24,28},{28,24},{1,5},{5... | collective-permute-start | bytes 331784 | tf_op jit(solution)/shard_map/ppermute | solution.py:32
  72.7 5.2 %collective-permute-start.21 = (f32[217,128]{1,0:T(8,128)S(1)}, f32[217,128]{1,0:T(8,128)S(1)}, u32[]{:S(2)}, u32[]{:S(2)}) collective-permute-start(f32[217,128]{1,0:T(8,128)S(1)} %fusion.417), channel_id=1, source_target_pairs={{0,4},{4,0},{8,12},{12,8},{16,20},{20,16},{24,28},{28,24},{1,5},{5... | collective-permute-start | bytes 333320 | tf_op jit(solution)/shard_map/ppermute | solution.py:32
  75.9 6.9 %collective-permute-start.17 = (f32[216,128]{1,0:T(8,128)S(1)}, f32[216,128]{1,0:T(8,128)S(1)}, u32[]{:S(2)}, u32[]{:S(2)}) collective-permute-start(f32[216,128]{1,0:T(8,128)S(1)} %add.323), channel_id=1, source_target_pairs={{0,8},{4,12},{8,0},{12,4},{16,24},{20,28},{24,16},{28,20},{1,9},{5... | collective-permute-start | bytes 331784 | tf_op jit(solution)/shard_map/ppermute | solution.py:32
  77.9 6.4 %collective-permute-start.22 = (f32[217,128]{1,0:T(8,128)S(1)}, f32[217,128]{1,0:T(8,128)S(1)}, u32[]{:S(2)}, u32[]{:S(2)}) collective-permute-start(f32[217,128]{1,0:T(8,128)S(1)} %add.329), channel_id=1, source_target_pairs={{0,8},{4,12},{8,0},{12,4},{16,24},{20,28},{24,16},{28,20},{1,9},{5... | collective-permute-start | bytes 333320 | tf_op jit(solution)/shard_map/ppermute | solution.py:32
  82.8 9.3 %collective-permute-start.18 = (f32[216,128]{1,0:T(8,128)S(1)}, f32[216,128]{1,0:T(8,128)S(1)}, u32[]{:S(2)}, u32[]{:S(2)}) collective-permute-start(f32[216,128]{1,0:T(8,128)S(1)} %add.324), channel_id=1, source_target_pairs={{0,16},{4,20},{8,24},{12,28},{16,0},{20,4},{24,8},{28,12},{1,17},{... | collective-permute-start | bytes 331784 | tf_op jit(solution)/shard_map/ppermute | solution.py:32
  84.4 8.9 %collective-permute-start.23 = (f32[217,128]{1,0:T(8,128)S(1)}, f32[217,128]{1,0:T(8,128)S(1)}, u32[]{:S(2)}, u32[]{:S(2)}) collective-permute-start(f32[217,128]{1,0:T(8,128)S(1)} %add.330), channel_id=1, source_target_pairs={{0,16},{4,20},{8,24},{12,28},{16,0},{20,4},{24,8},{28,12},{1,17},{... | collective-permute-start | bytes 333320 | tf_op jit(solution)/shard_map/ppermute | solution.py:32
  (7 other events, 39.0 us)

commit v3 on v1

--- a/solution.py
+++ b/solution.py
@@ -106,6 +106,10 @@
     depth_all = pre_first.shape[2] * count_los
     norm_factor = 1.0 / math.sqrt(features.shape[1] * count_sky * features.shape[3] * depth_all)
     shape = features.shape
+    saved_padded = wrap_columns(
+        extended(jnp.stack((features, pre_first)), (("sky", 2), ("los", 3)), 1)
+    )
+    hidden_padded = jax.nn.silu(saved_padded[1].astype(jnp.float32)).astype(jnp.bfloat16)
     first_wide = pre_first.astype(jnp.float32)
     second_wide = pre_second.astype(jnp.float32)
     hidden_second = jax.nn.silu(second_wide).astype(jnp.bfloat16)
@@ -137,23 +141,24 @@
     grad_bias = jnp.sum(head_grad.astype(jnp.float32), axis=(1, 2, 3)) * norm_factor
     back_second = jnp.einsum("oi,oxzy->ixzy", w_out, head_grad, preferred_element_type=jnp.float32)
     grad_second_pre = (back_second * silu_slope(second_wide)).astype(jnp.bfloat16)
+    grad_second = taps_from_inputs(grad_second_pre, hidden_padded)
+    early = (grad_second * norm_factor, grad_out, grad_bias)
+    early_shapes = [part.shape for part in early]
+    early_packed, grad_second_pre = lax.optimization_barrier((pack_rows(early), grad_second_pre))
+    early_packed = butterfly_sum(early_packed, ("los", "sky"))
     second_padded = wrap_columns(extended(grad_second_pre, (("sky", 1), ("los", 2)), 1))
     back_first = spread_local(w_second, second_padded, shape)
     grad_first_pre = (back_first * silu_slope(first_wide)).astype(jnp.bfloat16)
+    early_packed, grad_first_pre = lax.optimization_barrier((early_packed, grad_first_pre))
+    grad_first = taps_from_inputs(grad_first_pre, saved_padded[0])
+    late_packed, grad_first_pre = lax.optimization_barrier(
+        (pack_rows((grad_first * norm_factor,)), grad_first_pre)
+    )
+    late_packed = butterfly_sum(late_packed, ("los", "sky"))
     first_padded = wrap_columns(extended(grad_first_pre, (("sky", 1), ("los", 2)), 1))
     grad_features = spread_local(w_first, first_padded, shape).astype(jnp.bfloat16)
-    saved_padded = wrap_columns(
-        extended(jnp.stack((features, pre_first)), (("sky", 2), ("los", 3)), 1)
-    )
-    hidden_padded = jax.nn.silu(saved_padded[1].astype(jnp.float32)).astype(jnp.bfloat16)
-    grad_second = taps_from_inputs(grad_second_pre, hidden_padded)
-    grad_first = taps_from_inputs(grad_first_pre, saved_padded[0])
-    early = (grad_second * norm_factor, grad_out, grad_bias)
-    early_shapes = [part.shape for part in early]
-    grad_second, grad_out, grad_bias = unpack_rows(
-        butterfly_sum(pack_rows(early), ("los", "sky")), early_shapes
-    )
-    grad_first = butterfly_sum(grad_first * norm_factor, ("los", "sky"))
+    grad_second, grad_out, grad_bias = unpack_rows(early_packed, early_shapes)
+    (grad_first,) = unpack_rows(late_packed, [grad_first.shape])
     return (grad_features, grad_first, grad_second, grad_out, grad_bias)
 
 

time: 126 us -> 114 us (0.905)
  waiting for transfers between devices: 65.8 us -> 44.2 us
  starting transfers between devices: 21.4 us -> 31.9 us
    ppermute x12, waiting for transfers between devices: 51.8 us -> 31.1 us  [butterfly_sum(): value = value + lax.ppermute(value, axis, pairs)]
    ppermute x12, starting transfers between devices: 8.24 us -> 14.7 us  [butterfly_sum(): value = value + lax.ppermute(value, axis, pairs)]
    ppermute x6, waiting for transfers between devices: 4.6 us -> 1.37 us  [extended(): lax.ppermute(lax.slice_in_dim(block, 0, width, axis=dim), axis, backward)]
    ppermute x6, starting transfers between devices: 9.61 us -> 12.6 us  [extended(): lax.ppermute(lax.slice_in_dim(block, 0, width, axis=dim), axis, backward)]
    ppermute x6, waiting for transfers between devices: 9.45 us -> 11.7 us  [extended(): lax.ppermute(lax.slice_in_dim(block, block.shape[dim] - width, None, axis...]
    unnamed x17 -> x19, local copies, waits for them, and re-layouts: 3.7 us -> 1.66 us
    another operation x0 -> x2, local copies, waits for them, and re-layouts: none -> 1.96 us  [the longest x1 1.04 us: per_device(): jnp.stack((features, pre_first))]
  transfers between devices with their start and end apart: 24 -> 24, of which waited for: 14 -> 15; matrix products, arithmetic and copies ran while one was open for 25% -> 16% of each run, Pallas kernels for 0% -> 0%
where the time goes in v3:
time: 114 us
  waiting for transfers between devices  44.2 us (39%)
  starting transfers between devices  31.9 us (28%)
  matrix products  24.4 us (21%)
  local copies, waits for them, and re-layouts  7.02 us (6%)
  other arithmetic  4.59 us (4%)
  between operations  1.46 us (1%)
    ppermute x12, waiting for transfers between devices, butterfly_sum(): value = value + lax.ppermute(value, axis, pairs)  31.1 us
    ppermute x12, starting transfers between devices, butterfly_sum(): value = value + lax.ppermute(value, axis, pairs)  14.7 us
    ppermute x6, starting transfers between devices, extended(): lax.ppermute(lax.slice_in_dim(block, 0, width, axis=dim), axis, backward)  12.6 us
    dot_general x54, matrix products, spread_local(): jnp.einsum('oi,oxzy->ixzy', weight[tap_x, tap_z, tap_y], window, preferre...  12 us
    dot_general x54, matrix products, taps_from_inputs(): jnp.einsum('oxzy,ixzy->oi', grad_field, window, preferred_element_type=jn...  11.9 us
    ppermute x6, waiting for transfers between devices, extended(): lax.ppermute(lax.slice_in_dim(block, block.shape[dim] - width, None, axis...  11.7 us
    ppermute x6, starting transfers between devices, extended(): lax.ppermute(lax.slice_in_dim(block, block.shape[dim] - width, None, axis...  4.67 us
  transfers between devices with their start and end apart: 24, of which 15 were waited for; matrix products, arithmetic and copies ran while one was open for 16% of the time, Pallas kernels for 0%

profile of v3, /device:TPU:0, one launch (start us, length us, event | category | flops | bytes accessed | tf_op | source)
XLA Modules:
  0.0 113.6 jit_solution(939459078749154784)
XLA Ops:
  4.2 2.6 %collective-permute-start.1 = (f32[2,2,128]{2,1,0:T(2,128)S(1)}, f32[2,2,128]{2,1,0:T(2,128)S(1)}, u32[]{:S(2)}, u32[]{:S(2)}) collective-permute-start(f32[2,2,128]{2,1,0:T(2,128)S(1)} %fusion.372), channel_id=1, source_target_pairs={{0,2},{1,3},{2,0},{3,1},{4,6},{5,7},{6,4},{7,5},{8,10},{9,11},{10,... | collective-permute-start | bytes 6152 | tf_op jit(solution)/shard_map/ppermute | solution.py:32
  6.8 1.6 %collective-permute-start.2 = (bf16[2,32,1,8,128]{4,1,3,2,0:T(8,128)(2,1)S(1)}, bf16[2,32,1,8,128]{4,1,3,2,0:T(8,128)(2,1)S(1)}, u32[]{:S(2)}, u32[]{:S(2)}) collective-permute-start(bf16[2,32,1,8,128]{4,1,3,2,0:T(8,128)(2,1)S(1)} %get-tuple-element.52), channel_id=1, source_target_pairs={{0,4},{4,8},{8,12},{12,16},{16,20},{20,24},{24,28},{28,0},{1,5},{5... | collective-permute-start | bytes 393224 | tf_op jit(solution)/shard_map/ppermute | solution.py:15
  8.4 3.2 %collective-permute-start.3 = (bf16[2,32,1,8,128]{4,1,3,2,0:T(8,128)(2,1)S(1)}, bf16[2,32,1,8,128]{4,1,3,2,0:T(8,128)(2,1)S(1)}, u32[]{:S(2)}, u32[]{:S(2)}) collective-permute-start(bf16[2,32,1,8,128]{4,1,3,2,0:T(8,128)(2,1)S(1)} %get-tuple-element.53), channel_id=1, source_target_pairs={{4,0},{8,4},{12,8},{16,12},{20,16},{24,20},{28,24},{0,28},{5,1},{9... | collective-permute-start | bytes 393224 | tf_op jit(solution)/shard_map/ppermute | solution.py:18
  12.2 3.2 %collective-permute-done.2 = bf16[2,32,1,8,128]{4,1,3,2,0:T(8,128)(2,1)S(1)} collective-permute-done((bf16[2,32,1,8,128]{4,1,3,2,0:T(8,128)(2,1)S(1)}, bf16[2,32,1,8,128]{4,1,3,2,0:T(8,128)(2,1)S(1)}, u32[]{:S(2)}, u32[]{:S(2)}) %collective-permute-start.2) | collective-permute-done | bytes 131104 | tf_op jit(solution)/shard_map/ppermute | solution.py:15
  16.6 1.7 %collective-permute-start.5 = (bf16[2,32,4,1,128]{4,1,3,2,0:T(8,128)(2,1)S(1)}, bf16[2,32,4,1,128]{4,1,3,2,0:T(8,128)(2,1)S(1)}, u32[]{:S(2)}, u32[]{:S(2)}) collective-permute-start(bf16[2,32,4,1,128]{4,1,3,2,0:T(8,128)(2,1)S(1)} %get-tuple-element.39), channel_id=1, source_target_pairs={{1,0},{2,1},{3,2},{0,3},{5,4},{6,5},{7,6},{4,7},{9,8},{10,9},{11,1... | collective-permute-start | bytes 196616 | tf_op jit(solution)/shard_map/ppermute | solution.py:18
  18.4 1.9 %collective-permute-done.4 = bf16[2,32,4,1,128]{4,1,3,2,0:T(8,128)(2,1)S(1)} collective-permute-done((bf16[2,32,4,1,128]{4,1,3,2,0:T(8,128)(2,1)S(1)}, bf16[2,32,4,1,128]{4,1,3,2,0:T(8,128)(2,1)S(1)}, u32[]{:S(2)}, u32[]{:S(2)}) %collective-permute-start.4) | collective-permute-done | bytes 65568 | tf_op jit(solution)/shard_map/ppermute | solution.py:15
  28.5 4.5 %collective-permute-start.12 = (bf16[32,1,8,128]{3,0,2,1:T(8,128)(2,1)S(1)}, bf16[32,1,8,128]{3,0,2,1:T(8,128)(2,1)S(1)}, u32[]{:S(2)}, u32[]{:S(2)}) collective-permute-start(bf16[32,1,8,128]{3,0,2,1:T(8,128)(2,1)S(1)} %get-tuple-element.56), channel_id=1, source_target_pairs={{4,0},{8,4},{12,8},{16,12},{20,16},{24,20},{28,24},{0,28},{5,1},{9... | collective-permute-start | bytes 196616 | tf_op jit(solution)/shard_map/ppermute | solution.py:18
  33.0 2.6 %collective-permute-done.11 = bf16[32,1,8,128]{3,0,2,1:T(8,128)(2,1)S(1)} collective-permute-done((bf16[32,1,8,128]{3,0,2,1:T(8,128)(2,1)S(1)}, bf16[32,1,8,128]{3,0,2,1:T(8,128)(2,1)S(1)}, u32[]{:S(2)}, u32[]{:S(2)}) %collective-permute-start.11) | collective-permute-done | bytes 65568 | tf_op jit(solution)/shard_map/ppermute | solution.py:15
  37.6 1.8 %collective-permute-done.13 = bf16[32,4,1,128]{3,0,2,1:T(8,128)(2,1)S(1)} collective-permute-done((bf16[32,4,1,128]{3,0,2,1:T(8,128)(2,1)S(1)}, bf16[32,4,1,128]{3,0,2,1:T(8,128)(2,1)S(1)}, u32[]{:S(2)}, u32[]{:S(2)}) %collective-permute-start.13) | collective-permute-done | bytes 32800 | tf_op jit(solution)/shard_map/ppermute | solution.py:15
  45.8 1.2 %collective-permute-start.7 = (f32[217,128]{1,0:T(8,128)S(1)}, f32[217,128]{1,0:T(8,128)S(1)}, u32[]{:S(2)}, u32[]{:S(2)}) collective-permute-start(f32[217,128]{1,0:T(8,128)S(1)} %add.266), channel_id=1, source_target_pairs={{0,2},{1,3},{2,0},{3,1},{4,6},{5,7},{6,4},{7,5},{8,10},{9,11},{10,... | collective-permute-start | bytes 333320 | tf_op jit(solution)/shard_map/ppermute | solution.py:32
  47.2 3.5 %collective-permute-done.7 = f32[217,128]{1,0:T(8,128)S(1)} collective-permute-done((f32[217,128]{1,0:T(8,128)S(1)}, f32[217,128]{1,0:T(8,128)S(1)}, u32[]{:S(2)}, u32[]{:S(2)}) %collective-permute-start.7) | collective-permute-done | bytes 111136 | tf_op jit(solution)/shard_map/ppermute | solution.py:32
  51.9 3.7 %collective-permute-done.8 = f32[217,128]{1,0:T(8,128)S(1)} collective-permute-done((f32[217,128]{1,0:T(8,128)S(1)}, f32[217,128]{1,0:T(8,128)S(1)}, u32[]{:S(2)}, u32[]{:S(2)}) %collective-permute-start.8) | collective-permute-done | bytes 111136 | tf_op jit(solution)/shard_map/ppermute | solution.py:32
  55.6 1.2 %collective-permute-start.9 = (f32[217,128]{1,0:T(8,128)S(1)}, f32[217,128]{1,0:T(8,128)S(1)}, u32[]{:S(2)}, u32[]{:S(2)}) collective-permute-start(f32[217,128]{1,0:T(8,128)S(1)} %add.268), channel_id=1, source_target_pairs={{0,8},{4,12},{8,0},{12,4},{16,24},{20,28},{24,16},{28,20},{1,9},{5... | collective-permute-start | bytes 333320 | tf_op jit(solution)/shard_map/ppermute | solution.py:32
  57.1 3.4 %collective-permute-done.9 = f32[217,128]{1,0:T(8,128)S(1)} collective-permute-done((f32[217,128]{1,0:T(8,128)S(1)}, f32[217,128]{1,0:T(8,128)S(1)}, u32[]{:S(2)}, u32[]{:S(2)}) %collective-permute-start.9) | collective-permute-done | bytes 111136 | tf_op jit(solution)/shard_map/ppermute | solution.py:32
  60.5 3.1 %collective-permute-start.10 = (f32[217,128]{1,0:T(8,128)S(1)}, f32[217,128]{1,0:T(8,128)S(1)}, u32[]{:S(2)}, u32[]{:S(2)}) collective-permute-start(f32[217,128]{1,0:T(8,128)S(1)} %add.269), channel_id=1, source_target_pairs={{0,16},{4,20},{8,24},{12,28},{16,0},{20,4},{24,8},{28,12},{1,17},{... | collective-permute-start | bytes 333320 | tf_op jit(solution)/shard_map/ppermute | solution.py:32
  63.8 3.8 %collective-permute-done.10 = f32[217,128]{1,0:T(8,128)S(1)} collective-permute-done((f32[217,128]{1,0:T(8,128)S(1)}, f32[217,128]{1,0:T(8,128)S(1)}, u32[]{:S(2)}, u32[]{:S(2)}) %collective-permute-start.10) | collective-permute-done | bytes 111136 | tf_op jit(solution)/shard_map/ppermute | solution.py:32
  73.7 2.0 %collective-permute-start.15 = (bf16[32,1,8,128]{3,0,2,1:T(8,128)(2,1)S(1)}, bf16[32,1,8,128]{3,0,2,1:T(8,128)(2,1)S(1)}, u32[]{:S(2)}, u32[]{:S(2)}) collective-permute-start(bf16[32,1,8,128]{3,0,2,1:T(8,128)(2,1)S(1)} %get-tuple-element.55), channel_id=1, source_target_pairs={{0,4},{4,8},{8,12},{12,16},{16,20},{20,24},{24,28},{28,0},{1,5},{5... | collective-permute-start | bytes 196616 | tf_op jit(solution)/shard_map/ppermute | solution.py:15
  75.7 2.8 %collective-permute-start.16 = (bf16[32,1,8,128]{3,0,2,1:T(8,128)(2,1)S(1)}, bf16[32,1,8,128]{3,0,2,1:T(8,128)(2,1)S(1)}, u32[]{:S(2)}, u32[]{:S(2)}) collective-permute-start(bf16[32,1,8,128]{3,0,2,1:T(8,128)(2,1)S(1)} %get-tuple-element.54), channel_id=1, source_target_pairs={{4,0},{8,4},{12,8},{16,12},{20,16},{24,20},{28,24},{0,28},{5,1},{9... | collective-permute-start | bytes 196616 | tf_op jit(solution)/shard_map/ppermute | solution.py:18
  78.5 2.2 %collective-permute-done.15 = bf16[32,1,8,128]{3,0,2,1:T(8,128)(2,1)S(1)} collective-permute-done((bf16[32,1,8,128]{3,0,2,1:T(8,128)(2,1)S(1)}, bf16[32,1,8,128]{3,0,2,1:T(8,128)(2,1)S(1)}, u32[]{:S(2)}, u32[]{:S(2)}) %collective-permute-start.15) | collective-permute-done | bytes 65568 | tf_op jit(solution)/shard_map/ppermute | solution.py:15
  92.3 3.7 %collective-permute-done.20 = f32[216,128]{1,0:T(8,128)S(1)} collective-permute-done((f32[216,128]{1,0:T(8,128)S(1)}, f32[216,128]{1,0:T(8,128)S(1)}, u32[]{:S(2)}, u32[]{:S(2)}) %collective-permute-start.20) | collective-permute-done | bytes 110624 | tf_op jit(solution)/shard_map/ppermute | solution.py:32
  96.5 4.3 %collective-permute-done.21 = f32[216,128]{1,0:T(8,128)S(1)} collective-permute-done((f32[216,128]{1,0:T(8,128)S(1)}, f32[216,128]{1,0:T(8,128)S(1)}, u32[]{:S(2)}, u32[]{:S(2)}) %collective-permute-start.21) | collective-permute-done | bytes 110624 | tf_op jit(solution)/shard_map/ppermute | solution.py:32
  101.2 4.5 %collective-permute-done.22 = f32[216,128]{1,0:T(8,128)S(1)} collective-permute-done((f32[216,128]{1,0:T(8,128)S(1)}, f32[216,128]{1,0:T(8,128)S(1)}, u32[]{:S(2)}, u32[]{:S(2)}) %collective-permute-start.22) | collective-permute-done | bytes 110624 | tf_op jit(solution)/shard_map/ppermute | solution.py:32
  105.7 1.8 %collective-permute-start.23 = (f32[216,128]{1,0:T(8,128)S(1)}, f32[216,128]{1,0:T(8,128)S(1)}, u32[]{:S(2)}, u32[]{:S(2)}) collective-permute-start(f32[216,128]{1,0:T(8,128)S(1)} %add.330), channel_id=1, source_target_pairs={{0,16},{4,20},{8,24},{12,28},{16,0},{20,4},{24,8},{28,12},{1,17},{... | collective-permute-start | bytes 331784 | tf_op jit(solution)/shard_map/ppermute | solution.py:32
  108.5 4.1 %collective-permute-done.23 = f32[216,128]{1,0:T(8,128)S(1)} collective-permute-done((f32[216,128]{1,0:T(8,128)S(1)}, f32[216,128]{1,0:T(8,128)S(1)}, u32[]{:S(2)}, u32[]{:S(2)}) %collective-permute-start.23) | collective-permute-done | bytes 110624 | tf_op jit(solution)/shard_map/ppermute | solution.py:32
  (208 shorter events, 43.6 us)
Async XLA Ops:
  2.6 1.6 %collective-permute-start = (f32[2,2,128]{2,1,0:T(2,128)S(1)}, f32[2,2,128]{2,1,0:T(2,128)S(1)}, u32[]{:S(2)}, u32[]{:S(2)}) collective-permute-start(f32[2,2,128]{2,1,0:T(2,128)S(1)} %pad_maximum_fusion.28), channel_id=1, source_target_pairs={{0,1},{1,0},{2,3},{3,2},{4,5},{5,4},{6,7},{7,6},{8,9},{9,8},{10,11... | collective-permute-start | bytes 6152 | tf_op jit(solution)/shard_map/ppermute | solution.py:32
  4.2 7.4 %collective-permute-start.1 = (f32[2,2,128]{2,1,0:T(2,128)S(1)}, f32[2,2,128]{2,1,0:T(2,128)S(1)}, u32[]{:S(2)}, u32[]{:S(2)}) collective-permute-start(f32[2,2,128]{2,1,0:T(2,128)S(1)} %fusion.372), channel_id=1, source_target_pairs={{0,2},{1,3},{2,0},{3,1},{4,6},{5,7},{6,4},{7,5},{8,10},{9,11},{10,... | collective-permute-start | bytes 6152 | tf_op jit(solution)/shard_map/ppermute | solution.py:32
  6.8 8.6 %collective-permute-start.2 = (bf16[2,32,1,8,128]{4,1,3,2,0:T(8,128)(2,1)S(1)}, bf16[2,32,1,8,128]{4,1,3,2,0:T(8,128)(2,1)S(1)}, u32[]{:S(2)}, u32[]{:S(2)}) collective-permute-start(bf16[2,32,1,8,128]{4,1,3,2,0:T(8,128)(2,1)S(1)} %get-tuple-element.52), channel_id=1, source_target_pairs={{0,4},{4,8},{8,12},{12,16},{16,20},{20,24},{24,28},{28,0},{1,5},{5... | collective-permute-start | bytes 393224 | tf_op jit(solution)/shard_map/ppermute | solution.py:15
  8.4 8.1 %collective-permute-start.3 = (bf16[2,32,1,8,128]{4,1,3,2,0:T(8,128)(2,1)S(1)}, bf16[2,32,1,8,128]{4,1,3,2,0:T(8,128)(2,1)S(1)}, u32[]{:S(2)}, u32[]{:S(2)}) collective-permute-start(bf16[2,32,1,8,128]{4,1,3,2,0:T(8,128)(2,1)S(1)} %get-tuple-element.53), channel_id=1, source_target_pairs={{4,0},{8,4},{12,8},{16,12},{20,16},{24,20},{28,24},{0,28},{5,1},{9... | collective-permute-start | bytes 393224 | tf_op jit(solution)/shard_map/ppermute | solution.py:18
  16.6 3.7 %collective-permute-start.4 = (bf16[2,32,4,1,128]{4,1,3,2,0:T(8,128)(2,1)S(1)}, bf16[2,32,4,1,128]{4,1,3,2,0:T(8,128)(2,1)S(1)}, u32[]{:S(2)}, u32[]{:S(2)}) collective-permute-start(bf16[2,32,4,1,128]{4,1,3,2,0:T(8,128)(2,1)S(1)} %get-tuple-element.38), channel_id=1, source_target_pairs={{0,1},{1,2},{2,3},{3,0},{4,5},{5,6},{6,7},{7,4},{8,9},{9,10},{10,1... | collective-permute-start | bytes 196616 | tf_op jit(solution)/shard_map/ppermute | solution.py:15
  16.6 3.7 %collective-permute-start.5 = (bf16[2,32,4,1,128]{4,1,3,2,0:T(8,128)(2,1)S(1)}, bf16[2,32,4,1,128]{4,1,3,2,0:T(8,128)(2,1)S(1)}, u32[]{:S(2)}, u32[]{:S(2)}) collective-permute-start(bf16[2,32,4,1,128]{4,1,3,2,0:T(8,128)(2,1)S(1)} %get-tuple-element.39), channel_id=1, source_target_pairs={{1,0},{2,1},{3,2},{0,3},{5,4},{6,5},{7,6},{4,7},{9,8},{10,9},{11,1... | collective-permute-start | bytes 196616 | tf_op jit(solution)/shard_map/ppermute | solution.py:18
  28.2 7.4 %collective-permute-start.11 = (bf16[32,1,8,128]{3,0,2,1:T(8,128)(2,1)S(1)}, bf16[32,1,8,128]{3,0,2,1:T(8,128)(2,1)S(1)}, u32[]{:S(2)}, u32[]{:S(2)}) collective-permute-start(bf16[32,1,8,128]{3,0,2,1:T(8,128)(2,1)S(1)} %get-tuple-element.57), channel_id=1, source_target_pairs={{0,4},{4,8},{8,12},{12,16},{16,20},{20,24},{24,28},{28,0},{1,5},{5... | collective-permute-start | bytes 196616 | tf_op jit(solution)/shard_map/ppermute | solution.py:15
  28.5 7.1 %collective-permute-start.12 = (bf16[32,1,8,128]{3,0,2,1:T(8,128)(2,1)S(1)}, bf16[32,1,8,128]{3,0,2,1:T(8,128)(2,1)S(1)}, u32[]{:S(2)}, u32[]{:S(2)}) collective-permute-start(bf16[32,1,8,128]{3,0,2,1:T(8,128)(2,1)S(1)} %get-tuple-element.56), channel_id=1, source_target_pairs={{4,0},{8,4},{12,8},{16,12},{20,16},{24,20},{28,24},{0,28},{5,1},{9... | collective-permute-start | bytes 196616 | tf_op jit(solution)/shard_map/ppermute | solution.py:18
  35.6 1.9 %collective-permute-start.14 = (bf16[32,4,1,128]{3,0,2,1:T(8,128)(2,1)S(1)}, bf16[32,4,1,128]{3,0,2,1:T(8,128)(2,1)S(1)}, u32[]{:S(2)}, u32[]{:S(2)}) collective-permute-start(bf16[32,4,1,128]{3,0,2,1:T(8,128)(2,1)S(1)} %get-tuple-element.51), channel_id=1, source_target_pairs={{1,0},{2,1},{3,2},{0,3},{5,4},{6,5},{7,6},{4,7},{9,8},{10,9},{11,1... | collective-permute-start | bytes 98312 | tf_op jit(solution)/shard_map/ppermute | solution.py:18
  36.0 3.4 %collective-permute-start.13 = (bf16[32,4,1,128]{3,0,2,1:T(8,128)(2,1)S(1)}, bf16[32,4,1,128]{3,0,2,1:T(8,128)(2,1)S(1)}, u32[]{:S(2)}, u32[]{:S(2)}) collective-permute-start(bf16[32,4,1,128]{3,0,2,1:T(8,128)(2,1)S(1)} %get-tuple-element.50), channel_id=1, source_target_pairs={{0,1},{1,2},{2,3},{3,0},{4,5},{5,6},{6,7},{7,4},{8,9},{9,10},{10,1... | collective-permute-start | bytes 98312 | tf_op jit(solution)/shard_map/ppermute | solution.py:15
  36.2 9.5 %collective-permute-start.6 = (f32[217,128]{1,0:T(8,128)S(1)}, f32[217,128]{1,0:T(8,128)S(1)}, u32[]{:S(2)}, u32[]{:S(2)}) collective-permute-start(f32[217,128]{1,0:T(8,128)S(1)} %pad_bitcast_fusion), channel_id=1, source_target_pairs={{0,1},{1,0},{2,3},{3,2},{4,5},{5,4},{6,7},{7,6},{8,9},{9,8},{10,11... | collective-permute-start | bytes 333320 | tf_op jit(solution)/shard_map/ppermute | solution.py:32
  45.8 4.9 %collective-permute-start.7 = (f32[217,128]{1,0:T(8,128)S(1)}, f32[217,128]{1,0:T(8,128)S(1)}, u32[]{:S(2)}, u32[]{:S(2)}) collective-permute-start(f32[217,128]{1,0:T(8,128)S(1)} %add.266), channel_id=1, source_target_pairs={{0,2},{1,3},{2,0},{3,1},{4,6},{5,7},{6,4},{7,5},{8,10},{9,11},{10,... | collective-permute-start | bytes 333320 | tf_op jit(solution)/shard_map/ppermute | solution.py:32
  50.7 4.9 %collective-permute-start.8 = (f32[217,128]{1,0:T(8,128)S(1)}, f32[217,128]{1,0:T(8,128)S(1)}, u32[]{:S(2)}, u32[]{:S(2)}) collective-permute-start(f32[217,128]{1,0:T(8,128)S(1)} %add.267), channel_id=1, source_target_pairs={{0,4},{4,0},{8,12},{12,8},{16,20},{20,16},{24,28},{28,24},{1,5},{5... | collective-permute-start | bytes 333320 | tf_op jit(solution)/shard_map/ppermute | solution.py:32
  55.6 4.9 %collective-permute-start.9 = (f32[217,128]{1,0:T(8,128)S(1)}, f32[217,128]{1,0:T(8,128)S(1)}, u32[]{:S(2)}, u32[]{:S(2)}) collective-permute-start(f32[217,128]{1,0:T(8,128)S(1)} %add.268), channel_id=1, source_target_pairs={{0,8},{4,12},{8,0},{12,4},{16,24},{20,28},{24,16},{28,20},{1,9},{5... | collective-permute-start | bytes 333320 | tf_op jit(solution)/shard_map/ppermute | solution.py:32
  60.5 7.1 %collective-permute-start.10 = (f32[217,128]{1,0:T(8,128)S(1)}, f32[217,128]{1,0:T(8,128)S(1)}, u32[]{:S(2)}, u32[]{:S(2)}) collective-permute-start(f32[217,128]{1,0:T(8,128)S(1)} %add.269), channel_id=1, source_target_pairs={{0,16},{4,20},{8,24},{12,28},{16,0},{20,4},{24,8},{28,12},{1,17},{... | collective-permute-start | bytes 333320 | tf_op jit(solution)/shard_map/ppermute | solution.py:32
  73.7 7.0 %collective-permute-start.15 = (bf16[32,1,8,128]{3,0,2,1:T(8,128)(2,1)S(1)}, bf16[32,1,8,128]{3,0,2,1:T(8,128)(2,1)S(1)}, u32[]{:S(2)}, u32[]{:S(2)}) collective-permute-start(bf16[32,1,8,128]{3,0,2,1:T(8,128)(2,1)S(1)} %get-tuple-element.55), channel_id=1, source_target_pairs={{0,4},{4,8},{8,12},{12,16},{16,20},{20,24},{24,28},{28,0},{1,5},{5... | collective-permute-start | bytes 196616 | tf_op jit(solution)/shard_map/ppermute | solution.py:15
  75.7 5.1 %collective-permute-start.16 = (bf16[32,1,8,128]{3,0,2,1:T(8,128)(2,1)S(1)}, bf16[32,1,8,128]{3,0,2,1:T(8,128)(2,1)S(1)}, u32[]{:S(2)}, u32[]{:S(2)}) collective-permute-start(bf16[32,1,8,128]{3,0,2,1:T(8,128)(2,1)S(1)} %get-tuple-element.54), channel_id=1, source_target_pairs={{4,0},{8,4},{12,8},{16,12},{20,16},{24,20},{28,24},{0,28},{5,1},{9... | collective-permute-start | bytes 196616 | tf_op jit(solution)/shard_map/ppermute | solution.py:18
  80.8 3.7 %collective-permute-start.18 = (bf16[32,4,1,128]{3,0,2,1:T(8,128)(2,1)S(1)}, bf16[32,4,1,128]{3,0,2,1:T(8,128)(2,1)S(1)}, u32[]{:S(2)}, u32[]{:S(2)}) collective-permute-start(bf16[32,4,1,128]{3,0,2,1:T(8,128)(2,1)S(1)} %get-tuple-element.49), channel_id=1, source_target_pairs={{1,0},{2,1},{3,2},{0,3},{5,4},{6,5},{7,6},{4,7},{9,8},{10,9},{11,1... | collective-permute-start | bytes 98312 | tf_op jit(solution)/shard_map/ppermute | solution.py:18
  80.9 3.6 %collective-permute-start.17 = (bf16[32,4,1,128]{3,0,2,1:T(8,128)(2,1)S(1)}, bf16[32,4,1,128]{3,0,2,1:T(8,128)(2,1)S(1)}, u32[]{:S(2)}, u32[]{:S(2)}) collective-permute-start(bf16[32,4,1,128]{3,0,2,1:T(8,128)(2,1)S(1)} %get-tuple-element.48), channel_id=1, source_target_pairs={{0,1},{1,2},{2,3},{3,0},{4,5},{5,6},{6,7},{7,4},{8,9},{9,10},{10,1... | collective-permute-start | bytes 98312 | tf_op jit(solution)/shard_map/ppermute | solution.py:15
  81.6 9.4 %collective-permute-start.19 = (f32[216,128]{1,0:T(8,128)S(1)}, f32[216,128]{1,0:T(8,128)S(1)}, u32[]{:S(2)}, u32[]{:S(2)}) collective-permute-start(f32[216,128]{1,0:T(8,128)S(1)} %mul.102), channel_id=1, source_target_pairs={{0,1},{1,0},{2,3},{3,2},{4,5},{5,4},{6,7},{7,6},{8,9},{9,8},{10,11... | collective-permute-start | bytes 331784 | tf_op jit(solution)/shard_map/ppermute | solution.py:32
  91.0 5.0 %collective-permute-start.20 = (f32[216,128]{1,0:T(8,128)S(1)}, f32[216,128]{1,0:T(8,128)S(1)}, u32[]{:S(2)}, u32[]{:S(2)}) collective-permute-start(f32[216,128]{1,0:T(8,128)S(1)} %add.327), channel_id=1, source_target_pairs={{0,2},{1,3},{2,0},{3,1},{4,6},{5,7},{6,4},{7,5},{8,10},{9,11},{10,... | collective-permute-start | bytes 331784 | tf_op jit(solution)/shard_map/ppermute | solution.py:32
  96.1 4.8 %collective-permute-start.21 = (f32[216,128]{1,0:T(8,128)S(1)}, f32[216,128]{1,0:T(8,128)S(1)}, u32[]{:S(2)}, u32[]{:S(2)}) collective-permute-start(f32[216,128]{1,0:T(8,128)S(1)} %add.328), channel_id=1, source_target_pairs={{0,4},{4,0},{8,12},{12,8},{16,20},{20,16},{24,28},{28,24},{1,5},{5... | collective-permute-start | bytes 331784 | tf_op jit(solution)/shard_map/ppermute | solution.py:32
  100.9 4.8 %collective-permute-start.22 = (f32[216,128]{1,0:T(8,128)S(1)}, f32[216,128]{1,0:T(8,128)S(1)}, u32[]{:S(2)}, u32[]{:S(2)}) collective-permute-start(f32[216,128]{1,0:T(8,128)S(1)} %add.329), channel_id=1, source_target_pairs={{0,8},{4,12},{8,0},{12,4},{16,24},{20,28},{24,16},{28,20},{1,9},{5... | collective-permute-start | bytes 331784 | tf_op jit(solution)/shard_map/ppermute | solution.py:32
  105.7 6.9 %collective-permute-start.23 = (f32[216,128]{1,0:T(8,128)S(1)}, f32[216,128]{1,0:T(8,128)S(1)}, u32[]{:S(2)}, u32[]{:S(2)}) collective-permute-start(f32[216,128]{1,0:T(8,128)S(1)} %add.330), channel_id=1, source_target_pairs={{0,16},{4,20},{8,24},{12,28},{16,0},{20,4},{24,8},{28,12},{1,17},{... | collective-permute-start | bytes 331784 | tf_op jit(solution)/shard_map/ppermute | solution.py:32
  (7 other events, 53.8 us)
